TPU v7x, 128 devices: a whole 4x4x4 slice. The times are simulated.
128 devices in a mesh: req: 16 (over x, z), head: 8 (over y, core).
Axes of the slice: x: 4, y: 4, z: 4, core: 2. Of those that a mesh axis runs over, the one named last changes fastest.
Arguments:
- tokens: bfloat16 [16384, 1536], P('req', 'head'), may hold values from -6 to 6
- new_counts: int32 [16, 4], P('req'), may hold values from 1 to 512, 1024 in all within a row
- kv_cache: bfloat16 [64, 8, 7680, 128], P('req', 'head'), may hold values from -300 to 300
- norm_attn: float32 [1536], replicated, may hold values from 0.1 to 1.9
- query_weight: bfloat16 [1536, 8, 192], P(None, 'head'), may hold values from -0.15625 to 0.15625
- key_value_weight: bfloat16 [1536, 8, 128], P(None, 'head'), may hold values from -0.4375 to 0.4375
- output_weight: bfloat16 [8, 192, 1536], P('head'), may hold values from -0.15625 to 0.15625
- norm_moe: float32 [1536], replicated, may hold values from 0.1 to 1.9
- routes: int32 [16384, 8], P(('req', 'head')), may hold values from 0 to 31, all different within a row; in each aligned block of 128 rows (0 to 127, 128 to 255, ...) at most 64 rows name the same one
- route_gain: float32 [16384, 8], P(('req', 'head')), may hold values from 0.03 to 0.3
- w_gate_up: bfloat16 [32, 1536, 1024], P('req'), may hold values from -0.15625 to 0.15625
- w_down: bfloat16 [32, 512, 1536], P('req'), may hold values from -0.25 to 0.25
Outputs:
- mixed: bfloat16 [16384, 1536], P(('req', 'head'))
Inputs may be any that keep to these rules, and one draw needn't show every extreme that they name: `new_counts`: the 4 counts of one index of req sum to 1024, and one of them is exactly 512. `routes`: the 8 experts of a row differ. In each aligned block of 128 rows (the rows of one device) no expert is named more than 64 times, a bound that some block reaches.
All inputs are finite; a program needn't handle non-finite values.
Results may differ from a plain program's by a relative error of at most 0.019.
Values may be sent and summed in bfloat16 or wider, within the bound.
No kernel may reach another device: no remote copies, remote signals or barrier semaphores. Data moves between devices by JAX's collectives and lax.ppermute only.
A program may use at most 128 MiB of HBM per device.

v0:
```python
import math

import jax
import jax.numpy as jnp
from jax import lax
from jax.sharding import PartitionSpec as P

EXPERTS = 32
TOPK = 8
RATIO = 15


floor_score = -1e30


def norm_rows(value_rows, gain_row):
    mean_square = jnp.mean(value_rows * value_rows, axis=-1, keepdims=True)
    return value_rows * lax.rsqrt(mean_square + 1e-05) * gain_row


def rope_tables(position, head_size):
    half_size = head_size // 2
    inverse = jnp.exp(
        jnp.arange(half_size, dtype=jnp.float32) * (-2.0 * math.log(10000.0) / head_size)
    )
    angles = position.astype(jnp.float32)[:, None] * inverse[None, :]
    angles = jnp.concatenate([angles, angles], axis=1)
    return (jnp.cos(angles), jnp.sin(angles))


def rotate(vectors, cos_part, sin_part):
    half_size = vectors.shape[-1] // 2
    turned = jnp.concatenate([-vectors[..., half_size:], vectors[..., :half_size]], axis=-1)
    return vectors * cos_part + turned * sin_part


def request_layout(counts, token_count, cache_ratio):
    end_rows = jnp.cumsum(counts)
    starts = end_rows - counts
    row_ids = jnp.arange(token_count, dtype=jnp.int32)
    segment = jnp.sum((row_ids[:, None] >= end_rows[None, :]).astype(jnp.int32), axis=1)
    member = (segment[:, None] == jnp.arange(counts.shape[0], dtype=jnp.int32)[None, :]).astype(
        jnp.int32
    )
    row_begin = jnp.sum(member * starts[None, :], axis=1)
    own_count = jnp.sum(member * counts[None, :], axis=1)
    position = cache_ratio * own_count + row_ids - row_begin
    return (starts, position)


def project(normed, query_weight, key_value_weight, position):
    token_count, model_width = normed.shape
    kv_heads = key_value_weight.shape[1]
    head_size = key_value_weight.shape[2] // 2
    group_size = query_weight.shape[2] // head_size
    query = jnp.dot(
        normed, query_weight.reshape(model_width, -1), preferred_element_type=jnp.float32
    )
    query = query.reshape(token_count, kv_heads, group_size, head_size)
    keyval = jnp.dot(
        normed, key_value_weight.reshape(model_width, -1), preferred_element_type=jnp.float32
    )
    keyval = keyval.reshape(token_count, kv_heads, 2 * head_size)
    cos_part, sin_part = rope_tables(position, head_size)
    query = rotate(query, cos_part[:, None, None, :], sin_part[:, None, None, :]).astype(
        jnp.bfloat16
    )
    new_key = rotate(keyval[..., :head_size], cos_part[:, None, :], sin_part[:, None, :]).astype(
        jnp.bfloat16
    )
    new_value = keyval[..., head_size:].astype(jnp.bfloat16)
    return (query, new_key, new_value)


def absorb(carried, scores, usable, value_rows, pattern):
    highest, denominator, numerator = carried
    scores = jnp.where(usable, scores, floor_score)
    new_top = jnp.maximum(highest, jnp.max(scores, axis=-1))
    rescale = jnp.exp(highest - new_top)
    weights = jnp.where(usable, jnp.exp(scores - new_top[..., None]), 0.0)
    denominator = denominator * rescale + jnp.sum(weights, axis=-1)
    numerator = numerator * rescale[..., None] + jnp.einsum(
        pattern, weights.astype(jnp.bfloat16), value_rows, preferred_element_type=jnp.float32
    )
    return (new_top, denominator, numerator)


def local(
    tokens,
    new_counts,
    kv_cache,
    norm_attn,
    query_weight,
    key_value_weight,
    output_weight,
    norm_moe,
    routes,
    route_gain,
    w_gate_up,
    w_down,
):
    whole = lax.all_gather(tokens, "head", axis=1, tiled=True)
    token_count, model_width = whole.shape
    normed = norm_rows(whole.astype(jnp.float32), norm_attn).astype(jnp.bfloat16)
    counts = new_counts[0]
    starts, position = request_layout(counts, token_count, RATIO)
    query, new_key, new_value = project(normed, query_weight, key_value_weight, position)
    kv_heads, group_size, head_size = (query.shape[1], query.shape[2], query.shape[3])
    window = token_count // 2
    key_block = 3 * window
    score_scale = 1.0 / math.sqrt(head_size)
    stat_shape = (kv_heads, group_size, window)

    def one_request(which, result):
        row_begin = starts[which]
        count_here = counts[which]
        cached = RATIO * count_here
        win_start = jnp.minimum(row_begin, token_count - window)
        row_ids = win_start + jnp.arange(window, dtype=jnp.int32)
        inside = (row_ids >= row_begin) & (row_ids < row_begin + count_here)
        q_win = lax.dynamic_slice_in_dim(query, win_start, window, 0)
        k_win = lax.dynamic_slice_in_dim(new_key, win_start, window, 0)
        v_win = lax.dynamic_slice_in_dim(new_value, win_start, window, 0)
        p_win = lax.dynamic_slice_in_dim(position, win_start, window, 0)
        past = lax.dynamic_index_in_dim(kv_cache, which, 0, keepdims=False)

        def key_step(block_index, carried):
            key_piece = lax.dynamic_slice_in_dim(past, block_index * key_block, key_block, 1)
            slot_ids = block_index * key_block + jnp.arange(key_block, dtype=jnp.int32)
            usable = (slot_ids < cached)[None, None, None, :]
            scores = (
                jnp.einsum(
                    "qhgd,hkd->hgqk",
                    q_win,
                    key_piece[..., :head_size],
                    preferred_element_type=jnp.float32,
                )
                * score_scale
            )
            return absorb(carried, scores, usable, key_piece[..., head_size:], "hgqk,hkd->hgqd")

        start_state = (
            jnp.full(stat_shape, floor_score, jnp.float32),
            jnp.zeros(stat_shape, jnp.float32),
            jnp.zeros(stat_shape + (head_size,), jnp.float32),
        )
        block_count = (cached + key_block - 1) // key_block
        carried = lax.fori_loop(0, block_count, key_step, start_state)
        new_ok = (inside[None, :] & (p_win[None, :] <= p_win[:, None]))[None, None, :, :]
        scores = (
            jnp.einsum("qhgd,khd->hgqk", q_win, k_win, preferred_element_type=jnp.float32)
            * score_scale
        )
        highest, denominator, numerator = absorb(carried, scores, new_ok, v_win, "hgqk,khd->hgqd")
        attended = jnp.transpose(numerator / denominator[..., None], (2, 0, 1, 3))
        current = lax.dynamic_slice_in_dim(result, win_start, window, 0)
        update = jnp.where(inside[:, None, None, None], attended, current)
        return lax.dynamic_update_slice_in_dim(result, update, win_start, 0)

    initial = jnp.zeros(query.shape, jnp.float32)
    result = lax.fori_loop(0, counts.shape[0], one_request, initial)
    attn_out = result.astype(jnp.bfloat16).reshape(token_count, -1)
    partial_value = jnp.dot(
        attn_out, output_weight.reshape(-1, model_width), preferred_element_type=jnp.float32
    )
    per_block = routes.shape[0]
    row_start = lax.axis_index("head") * per_block
    summed = lax.psum(partial_value.astype(jnp.bfloat16), "head").astype(jnp.float32)
    attn_rows = lax.dynamic_slice_in_dim(summed, row_start, per_block, 0)
    base_rows = lax.dynamic_slice_in_dim(whole, row_start, per_block, 0)
    resid = base_rows.astype(jnp.float32) + attn_rows
    moe_in = norm_rows(resid, norm_moe).astype(jnp.bfloat16)
    capacity = per_block // 2
    flat_routes = routes.reshape(-1)
    expert_ids = jnp.arange(EXPERTS, dtype=jnp.int32)
    onehot = (flat_routes[:, None] == expert_ids[None, :]).astype(jnp.int32)
    before = jnp.cumsum(onehot, axis=0) - onehot
    rank_in = jnp.sum(before * onehot, axis=1)
    slot_ids = flat_routes * capacity + rank_in
    owners = jnp.arange(per_block * TOPK, dtype=jnp.int32) // TOPK
    table = jnp.full((EXPERTS * capacity,), per_block, jnp.int32).at[slot_ids].set(owners)
    padded = jnp.concatenate([moe_in, jnp.zeros((1, model_width), jnp.bfloat16)], axis=0)
    req_count = lax.axis_size("req")
    per_req = w_down.shape[0]
    ff_width = w_down.shape[1]
    outgoing = padded[table].reshape(req_count, per_req, capacity, model_width)
    gate_up = jnp.einsum(
        "sncd,ndf->sncf",
        lax.all_to_all(outgoing, "req", split_axis=0, concat_axis=0, tiled=True),
        w_gate_up,
        preferred_element_type=jnp.float32,
    )
    hidden = (jax.nn.silu(gate_up[..., :ff_width]) * gate_up[..., ff_width:]).astype(jnp.bfloat16)
    produced = jnp.einsum(
        "sncf,nfd->sncd", hidden, w_down, preferred_element_type=jnp.float32
    ).astype(jnp.bfloat16)
    arrived = lax.all_to_all(produced, "req", split_axis=0, concat_axis=0, tiled=True)
    gathered = arrived.reshape(EXPERTS * capacity, model_width)[slot_ids].astype(jnp.float32)
    gathered = gathered.reshape(per_block, TOPK, model_width)
    moe_sum = jnp.sum(gathered * route_gain[..., None], axis=1)
    return (resid + moe_sum).astype(jnp.bfloat16)


def solution(mesh):
    in_specs = (
        P("req", "head"),
        P("req", None),
        P("req", "head", None, None),
        P(),
        P(None, "head", None),
        P(None, "head", None),
        P("head", None, None),
        P(),
        P(("req", "head"), None),
        P(("req", "head"), None),
        P("req", None, None),
        P("req", None, None),
    )
    out_specs = P(("req", "head"), None)
    return jax.shard_map(local, mesh=mesh, in_specs=in_specs, out_specs=out_specs, check_vma=False)
```

profile of v0, /device:TPU:93, one launch (start us, length us, event | category | flops | bytes accessed | tf_op | source)
XLA Modules:
  0.0 637.8 jit_solution(5013867156348235563)
XLA Ops:
  14.4 23.0 %all-gather.2.cloned.1.call-done = bf16[1024,1536]{0,1:T(8,128)(2,1)} async-done(((bf16[1024,192]{0,1:T(8,128)(2,1)}), bf16[1024,1536]{0,1:T(8,128)(2,1)}) %all-gather.2.cloned.1.call-update) | async-done | bytes 3145744 | tf_op jit(solution)/shard_map/all_gather | solution.py:102
  40.0 3.1 convolution_bitcast_fusion
  47.8 244.3 %while.88 = (s32[]{:T(128)}, bf16[1024,1,3,64]{0,3,2,1:T(8,128)(2,1)}, s32[4]{0:T(128)S(1)}, s32[4]{0:T(128)S(1)}, bf16[4,1,7680,128]{3,2,1,0:T(8,128)(2,1)}, /*...) while((s32[]{:T(128)}, ...), condition=%wide.region_12.13_spmd, body=%wide.region_5.12_spmd.sunk | while | flops 847329280 | bytes 89355064 | solution.py:161
  52.2 3.4 fusion.123
  56.3 3.0 constant_dynamic-slice_fusion.6
  59.2 4.0 copy.67
  65.1 12.6 %while.89 = (s32[]{:T(128)}, f32[1,3,512]{2,1,0:T(4,128)S(1)}, f32[1,3,512]{2,1,0:T(4,128)S(1)}, f32[1,3,512,64]{2,3,1,0:T(8,128)}, s32[]{:T(128)}, /*index=5*/s...) while((s32[]{:T(128)}, f32[1,3,512]{2,1,0:T(4,128)S(1)}, ...), condition=%wide.region_9.9_spmd, body=%wide.region_6.8_spmd.sunk | while | flops 634854912 | bytes 67547888 | solution.py:148
  71.6 6.1 fusion.131
  80.4 3.1 fusion.127
  83.6 3.3 dynamic_update_slice.15
  91.3 3.4 fusion.123
  95.3 3.0 constant_dynamic-slice_fusion.6
  98.3 4.0 copy.67
  104.2 25.2 %while.89 = (s32[]{:T(128)}, f32[1,3,512]{2,1,0:T(4,128)S(1)}, f32[1,3,512]{2,1,0:T(4,128)S(1)}, f32[1,3,512,64]{2,3,1,0:T(8,128)}, s32[]{:T(128)}, /*index=5*/s...) while((s32[]{:T(128)}, f32[1,3,512]{2,1,0:T(4,128)S(1)}, ...), condition=%wide.region_9.9_spmd, body=%wide.region_6.8_spmd.sunk | while | flops 634854912 | bytes 67547888 | solution.py:148
  110.7 6.1 fusion.131
  123.3 6.1 fusion.131
  132.1 3.1 fusion.127
  135.2 3.6 dynamic_update_slice.15
  143.3 3.4 fusion.123
  150.3 4.0 copy.67
  156.2 62.9 %while.89 = (s32[]{:T(128)}, f32[1,3,512]{2,1,0:T(4,128)S(1)}, f32[1,3,512]{2,1,0:T(4,128)S(1)}, f32[1,3,512,64]{2,3,1,0:T(8,128)}, s32[]{:T(128)}, /*index=5*/s...) while((s32[]{:T(128)}, f32[1,3,512]{2,1,0:T(4,128)S(1)}, ...), condition=%wide.region_9.9_spmd, body=%wide.region_6.8_spmd.sunk | while | flops 634854912 | bytes 67547888 | solution.py:148
  162.7 6.1 fusion.131
  175.2 6.1 fusion.131
  187.8 6.1 fusion.131
  200.4 6.1 fusion.131
  213.0 6.1 fusion.131
  221.8 3.1 fusion.127
  224.9 3.5 dynamic_update_slice.15
  232.9 3.4 fusion.123
  239.9 4.0 copy.67
  245.8 37.7 %while.89 = (s32[]{:T(128)}, f32[1,3,512]{2,1,0:T(4,128)S(1)}, f32[1,3,512]{2,1,0:T(4,128)S(1)}, f32[1,3,512,64]{2,3,1,0:T(8,128)}, s32[]{:T(128)}, /*index=5*/s...) while((s32[]{:T(128)}, f32[1,3,512]{2,1,0:T(4,128)S(1)}, ...), condition=%wide.region_9.9_spmd, body=%wide.region_6.8_spmd.sunk | while | flops 634854912 | bytes 67547888 | solution.py:148
  252.3 6.1 fusion.131
  264.9 6.1 fusion.131
  277.5 6.1 fusion.131
  286.3 3.1 fusion.127
  292.1 3.9 convolution_convert_fusion
  296.2 9.0 %reduce-window.11 = s32[32,8,128]{2,1,0:T(8,128)S(1)} reduce-window(s32[32,8,128]{2,1,0:T(8,128)S(1)} %fusion.96, s32[]{:T(128)} %constant.233.clone.1), window={size=1x1x128 pad=0_0x0_0x127_0}, to_apply=%region_15.16 | reduce-window | flops 4161536 | bytes 262148 | tf_op jit(solution)/shard_map/reduce-window.1
  305.8 4.3 scatter_custom_fusion
  313.0 64.0 %all-reduce.3.cloned.1.call-done = bf16[1024,1536]{1,0:T(8,128)(2,1)} async-done(((bf16[1024,1536]{1,0:T(8,128)(2,1)}), bf16[1024,1536]{1,0:T(8,128)(2,1)}) %all-reduce.3.cloned.1.call-update) | async-done | bytes 3145744 | tf_op jit(solution)/shard_map/psum | solution.py:168
  380.3 14.3 %gather_fusion = bf16[2048,1536]{1,0:T(8,128)(2,1)} fusion(bf16[129,1536]{1,0:T(8,128)(2,1)} %concatenate.59, s32[2048]{0:T(1024)S(1)} %fusion.98), kind=kCustom, calls=%fused_computation | custom fusion | bytes 12591104 | tf_op jit(solution)/shard_map/gather | solution.py:186
  394.6 76.3 %all_to_all.10 = bf16[16,2,64,1536]{3,2,1,0:T(8,128)(2,1)S(1)} all-to-all(bf16[16,2,64,1536]{3,2,1,0:T(8,128)(2,1)} %bitcast.290), channel_id=1, replica_groups=mesh['req'=16,'head'=8] {'req'}, dimensions={0} | all-to-all | bytes 12582912 | tf_op jit(solution)/shard_map/all_to_all | solution.py:189
  470.9 10.7 %fusion.70 = f32[16,2,64,1024]{3,2,0,1:T(8,128)} fusion(bf16[2,1536,1024]{2,1,0:T(8,128)(2,1)} %param.26, bf16[16,2,64,1536]{3,2,1,0:T(8,128)(2,1)S(1)} %all_to_all.10), kind=kOutput, calls=%fused_computation.81 | convolution fusion | flops 6442450944 | bytes 20971520 | tf_op jit(solution)/shard_map/sncd,ndf->sncf/dot_general | solution.py:187
  481.6 7.3 %convert_bitcast_fusion = bf16[16,2,64,1536]{3,2,0,1:T(8,128)(2,1)S(1)} fusion(bf16[2,512,1536]{2,1,0:T(8,128)(2,1)S(1)} %copy-done, f32[16,2,64,1024]{3,2,0,1:T(8,128)} %fusion.70), kind=kOutput, calls=%fused_computation.77 | convolution fusion | flops 3230662656 | bytes 17825792 | tf_op jit(solution)/shard_map/sncf,nfd->sncd/dot_general | solution.py:194
  488.9 3.1 copy.52
  492.1 8.1 %all-to-all-start.1 = ((bf16[16,2,64,1536]{3,2,1,0:T(8,128)(2,1)}), bf16[16,2,64,1536]{3,2,1,0:T(8,128)(2,1)}, u32[]{:S(2)}, u32[]{:S(2)}) async-start(bf16[16,2,64,1536]{3,2,1,0:T(8,128)(2,1)} %copy.52), calls=%async_computation.1 | async-start | bytes 12582912 | tf_op jit(solution)/shard_map/all_to_all | solution.py:197
  500.9 112.6 %all-to-all-done.1 = bf16[16,2,64,1536]{3,2,1,0:T(8,128)(2,1)} async-done(((bf16[16,2,64,1536]{3,2,1,0:T(8,128)(2,1)}), bf16[16,2,64,1536]{3,2,1,0:T(8,128)(2,1)}, u32[]{:S(2)}, u32[]{:S(2)}) %all-to-all-start.1) | async-done | bytes 6291488 | tf_op jit(solution)/shard_map/all_to_all | solution.py:197
  613.4 10.9 %gather_fusion.1 = bf16[1024,1536]{1,0:T(8,128)(2,1)} fusion(bf16[2048,1536]{1,0:T(8,128)(2,1)} %bitcast.54, s32[1024]{0:T(1024)S(1)} %broadcast_clamp_fusion), kind=kCustom, calls=%fused_computation.1 | custom fusion | bytes 6295552 | tf_op jit(solution)/shard_map/gather | solution.py:198
  624.4 4.7 fusion.65
  (217 shorter events, 132.9 us)
Async XLA Ops:
  6.5 475.1 %copy-start = (bf16[2,512,1536]{2,1,0:T(8,128)(2,1)S(1)}, bf16[2,512,1536]{2,1,0:T(8,128)(2,1)}, u32[]{:S(2)}) copy-start(bf16[2,512,1536]{2,1,0:T(8,128)(2,1)} %param.27) | copy-start | bytes 9437188
  6.5 33.5 %copy-start.12 = (f32[1536]{0:T(1024)S(1)}, f32[1536]{0:T(1024)}, u32[]{:S(2)}) copy-start(f32[1536]{0:T(1024)} %param.19) | copy-start | bytes 18436
  6.5 30.9 %all-gather.2.cloned.1.call-start = ((), (), s32[]{:S(2)}) async-start(), calls=%async_computation.2 | async-start | bytes 3538944 | tf_op jit(solution)/shard_map/all_gather | solution.py:102
  7.3 369.8 %all-reduce.3.cloned.1.call-start = ((), (), s32[]{:S(2)}) async-start(), calls=%async_computation.3 | async-start | bytes 6291456 | tf_op jit(solution)/shard_map/psum | solution.py:168
  40.0 3.9 copy-start.3
  40.0 3.9 copy-start.11
  43.9 2.1 copy-start.4
  43.9 2.1 copy-start.5
  44.9 2.8 copy-start.10
  51.5 0.7 copy-start.2
  68.0 3.6 copy-start.1
  90.6 0.7 copy-start.2
  107.0 3.6 copy-start.1
  119.6 3.6 copy-start.1
  142.6 0.7 copy-start.2
  159.0 3.6 copy-start.1
  171.6 3.6 copy-start.1
  184.2 3.6 copy-start.1
  196.7 3.6 copy-start.1
  209.3 3.6 copy-start.1
  232.2 0.7 copy-start.2
  248.6 3.6 copy-start.1
  261.2 3.6 copy-start.1
  273.8 3.6 copy-start.1
  292.0 3.9 copy-start.8
  292.0 4.1 copy-start.7
  292.1 13.6 %copy-start.6 = (s32[1024]{0:T(1024)S(1)}, s32[1024]{0:T(1024)}, u32[]{:S(2)}) copy-start(s32[1024]{0:T(1024)} %eq.41) | copy-start | bytes 12292
  492.1 8.1 %copy-start.9 = (f32[128,8]{0,1:T(8,128)S(1)}, f32[128,8]{0,1:T(8,128)}, u32[]{:S(2)}) copy-start(f32[128,8]{0,1:T(8,128)} %param.25) | copy-start | bytes 12292
  492.1 121.4 %all-to-all-start.1 = ((bf16[16,2,64,1536]{3,2,1,0:T(8,128)(2,1)}), bf16[16,2,64,1536]{3,2,1,0:T(8,128)(2,1)}, u32[]{:S(2)}, u32[]{:S(2)}) async-start(bf16[16,2,64,1536]{3,2,1,0:T(8,128)(2,1)} %copy.52), calls=%async_computation.1 | async-start | bytes 12582912 | tf_op jit(solution)/shard_map/all_to_all | solution.py:197
Sparse Core Ops, SparseCore 0:
  9.0 28.3 all-gather.1
  296.1 80.9 all-reduce.2
where the time goes:
time: 640 us; the launch traced here: 638 us
  waiting for transfers between devices  200 us (31%)
  matrix products  150 us (23%)
  local copies, waits for them, and re-layouts  105 us (16%)
  blocking collectives  76.3 us (12%)
  other arithmetic  73.7 us (12%)
  between operations  13.7 us (2%)
  loops' own time  10.2 us (2%)
  starting transfers between devices  8.1 us (1%)
    all_to_all x1, waiting for transfers between devices, local(): lax.all_to_all(produced, 'req', split_axis=0, concat_axis=0, tiled=True)  113 us
    dot_general x15, matrix products, absorb(): jnp.einsum(pattern, weights.astype(jnp.bfloat16), value_rows, preferred_e...  79.6 us
    all_to_all x1, blocking collectives, local(): lax.all_to_all(outgoing, 'req', split_axis=0, concat_axis=0, tiled=True)  76.3 us
    psum x1, waiting for transfers between devices, local(): lax.psum(partial_value.astype(jnp.bfloat16), 'head').astype(jnp.float32)  64 us
    reduce_sum x15, other arithmetic, absorb(): denominator = denominator * rescale + jnp.sum(weights, axis=-1)  42.5 us
    dot_general x11, matrix products, key_step(): jnp.einsum('qhgd,hkd->hgqk', q_win, key_piece[..., :head_size], preferred...  30.8 us
    dynamic_slice x8, local copies, waits for them, and re-layouts, one_request(): past = lax.dynamic_index_in_dim(kv_cache, which, 0, keepdims=False)  27.9 us
    all_gather x1, waiting for transfers between devices, local(): whole = lax.all_gather(tokens, 'head', axis=1, tiled=True)  23 us
  transfers between devices with their start and end apart: 3, of which 3 were waited for; matrix products, arithmetic and copies ran while one was open for 4% of the time, Pallas kernels for 0%

commit v1 on v0

--- a/solution.py
+++ b/solution.py
@@ -3,11 +3,16 @@
 import jax
 import jax.numpy as jnp
 from jax import lax
+from jax.experimental import pallas as pl
+from jax.experimental.pallas import tpu as pltpu
 from jax.sharding import PartitionSpec as P
 
 EXPERTS = 32
 TOPK = 8
 RATIO = 15
+WIN = 512
+TQ = 256
+TK = 1536
 
 
 floor_score = -1e30
@@ -72,17 +77,101 @@
     return (query, new_key, new_value)
 
 
-def absorb(carried, scores, usable, value_rows, pattern):
-    highest, denominator, numerator = carried
-    scores = jnp.where(usable, scores, floor_score)
-    new_top = jnp.maximum(highest, jnp.max(scores, axis=-1))
-    rescale = jnp.exp(highest - new_top)
-    weights = jnp.where(usable, jnp.exp(scores - new_top[..., None]), 0.0)
-    denominator = denominator * rescale + jnp.sum(weights, axis=-1)
-    numerator = numerator * rescale[..., None] + jnp.einsum(
-        pattern, weights.astype(jnp.bfloat16), value_rows, preferred_element_type=jnp.float32
-    )
-    return (new_top, denominator, numerator)
+def attn_kernel(counts_ref, q_ref, kv_ref, nkv_ref, o_ref, m_sc, l_sc, acc_sc):
+    j = pl.program_id(0)
+    qi = pl.program_id(1)
+    kb = pl.program_id(2)
+    last = pl.num_programs(2) - 1
+    count = counts_ref[j]
+    groups, tq, width = q_ref.shape[1], q_ref.shape[2], q_ref.shape[3]
+    tk = kv_ref.shape[2]
+    win = nkv_ref.shape[1]
+    scale = 1.0 / math.sqrt(width // 2)
+    tile_ok = qi * tq < count
+
+    @pl.when(kb == 0)
+    def _():
+        m_sc[...] = jnp.full(m_sc.shape, floor_score, jnp.float32)
+        l_sc[...] = jnp.zeros(l_sc.shape, jnp.float32)
+        acc_sc[...] = jnp.zeros(acc_sc.shape, jnp.float32)
+
+    def absorb(rows, mask):
+        q = q_ref[0].reshape(groups * tq, width)
+        s = lax.dot_general(
+            q, rows, (((1,), (1,)), ((), ())), preferred_element_type=jnp.float32
+        )
+        s = (s * scale).reshape(groups, tq, rows.shape[0])
+        s = jnp.where(mask, s, floor_score)
+        m_old = m_sc[...]
+        m_new = jnp.maximum(m_old, jnp.max(s, axis=-1, keepdims=True))
+        alpha = jnp.exp(m_old - m_new)
+        p = jnp.where(mask, jnp.exp(s - m_new), 0.0)
+        l_sc[...] = l_sc[...] * alpha + jnp.sum(p, axis=-1, keepdims=True)
+        pv = jnp.dot(
+            p.astype(jnp.bfloat16).reshape(groups * tq, rows.shape[0]),
+            rows,
+            preferred_element_type=jnp.float32,
+        )
+        acc_sc[...] = acc_sc[...] * alpha + pv.reshape(groups, tq, width)
+        m_sc[...] = m_new
+
+    @pl.when(tile_ok & (kb == 0))
+    def _():
+        row = qi * tq + lax.broadcasted_iota(jnp.int32, (1, tq, win), 1)
+        col = lax.broadcasted_iota(jnp.int32, (1, tq, win), 2)
+        absorb(nkv_ref[0], col <= row)
+
+    @pl.when(tile_ok & (kb > 0) & ((kb - 1) * tk < RATIO * count))
+    def _():
+        col = (kb - 1) * tk + lax.broadcasted_iota(jnp.int32, (1, 1, tk), 2)
+        absorb(kv_ref[0, 0], col < RATIO * count)
+
+    @pl.when(kb == last)
+    def _():
+        total = l_sc[...]
+        total = jnp.where(total > 0.0, total, 1.0)
+        o_ref[0] = (acc_sc[...] / total).astype(o_ref.dtype)
+
+
+def attention(counts, q_win, kv_cache, nkv_win):
+    req_n, groups, win, width = q_win.shape
+    cache_len = kv_cache.shape[2]
+    n_tiles = win // TQ
+    n_blocks = cache_len // TK
+
+    def q_map(j, qi, kb, cnt):
+        tiles = (cnt[j] + TQ - 1) // TQ
+        return (j, 0, jnp.minimum(qi, tiles - 1), 0)
+
+    def kv_map(j, qi, kb, cnt):
+        tiles = (cnt[j] + TQ - 1) // TQ
+        blocks = (RATIO * cnt[j] + TK - 1) // TK
+        inner = jnp.clip(kb - 1, 0, blocks - 1)
+        return (j, 0, jnp.where(qi < tiles, inner, blocks - 1), 0)
+
+    grid_spec = pltpu.PrefetchScalarGridSpec(
+        num_scalar_prefetch=1,
+        grid=(req_n, n_tiles, n_blocks + 1),
+        in_specs=[
+            pl.BlockSpec((1, groups, TQ, width), q_map),
+            pl.BlockSpec((1, 1, TK, width), kv_map),
+            pl.BlockSpec((1, win, width), lambda j, qi, kb, cnt: (j, 0, 0)),
+        ],
+        out_specs=pl.BlockSpec((1, groups, TQ, width), lambda j, qi, kb, cnt: (j, 0, qi, 0)),
+        scratch_shapes=[
+            pltpu.VMEM((groups, TQ, 1), jnp.float32),
+            pltpu.VMEM((groups, TQ, 1), jnp.float32),
+            pltpu.VMEM((groups, TQ, width), jnp.float32),
+        ],
+    )
+    return pl.pallas_call(
+        attn_kernel,
+        grid_spec=grid_spec,
+        out_shape=jax.ShapeDtypeStruct(q_win.shape, jnp.bfloat16),
+        compiler_params=pltpu.CompilerParams(
+            dimension_semantics=("arbitrary", "arbitrary", "arbitrary")
+        ),
+    )(counts, q_win, kv_cache, nkv_win)
 
 
 def local(
@@ -105,68 +194,39 @@
     counts = new_counts[0]
     starts, position = request_layout(counts, token_count, RATIO)
     query, new_key, new_value = project(normed, query_weight, key_value_weight, position)
-    kv_heads, group_size, head_size = (query.shape[1], query.shape[2], query.shape[3])
-    window = token_count // 2
-    key_block = 3 * window
-    score_scale = 1.0 / math.sqrt(head_size)
-    stat_shape = (kv_heads, group_size, window)
-
-    def one_request(which, result):
-        row_begin = starts[which]
-        count_here = counts[which]
-        cached = RATIO * count_here
-        win_start = jnp.minimum(row_begin, token_count - window)
-        row_ids = win_start + jnp.arange(window, dtype=jnp.int32)
-        inside = (row_ids >= row_begin) & (row_ids < row_begin + count_here)
-        q_win = lax.dynamic_slice_in_dim(query, win_start, window, 0)
-        k_win = lax.dynamic_slice_in_dim(new_key, win_start, window, 0)
-        v_win = lax.dynamic_slice_in_dim(new_value, win_start, window, 0)
-        p_win = lax.dynamic_slice_in_dim(position, win_start, window, 0)
-        past = lax.dynamic_index_in_dim(kv_cache, which, 0, keepdims=False)
-
-        def key_step(block_index, carried):
-            key_piece = lax.dynamic_slice_in_dim(past, block_index * key_block, key_block, 1)
-            slot_ids = block_index * key_block + jnp.arange(key_block, dtype=jnp.int32)
-            usable = (slot_ids < cached)[None, None, None, :]
-            scores = (
-                jnp.einsum(
-                    "qhgd,hkd->hgqk",
-                    q_win,
-                    key_piece[..., :head_size],
-                    preferred_element_type=jnp.float32,
-                )
-                * score_scale
-            )
-            return absorb(carried, scores, usable, key_piece[..., head_size:], "hgqk,hkd->hgqd")
-
-        start_state = (
-            jnp.full(stat_shape, floor_score, jnp.float32),
-            jnp.zeros(stat_shape, jnp.float32),
-            jnp.zeros(stat_shape + (head_size,), jnp.float32),
-        )
-        block_count = (cached + key_block - 1) // key_block
-        carried = lax.fori_loop(0, block_count, key_step, start_state)
-        new_ok = (inside[None, :] & (p_win[None, :] <= p_win[:, None]))[None, None, :, :]
-        scores = (
-            jnp.einsum("qhgd,khd->hgqk", q_win, k_win, preferred_element_type=jnp.float32)
-            * score_scale
-        )
-        highest, denominator, numerator = absorb(carried, scores, new_ok, v_win, "hgqk,khd->hgqd")
-        attended = jnp.transpose(numerator / denominator[..., None], (2, 0, 1, 3))
-        current = lax.dynamic_slice_in_dim(result, win_start, window, 0)
-        update = jnp.where(inside[:, None, None, None], attended, current)
-        return lax.dynamic_update_slice_in_dim(result, update, win_start, 0)
-
-    initial = jnp.zeros(query.shape, jnp.float32)
-    result = lax.fori_loop(0, counts.shape[0], one_request, initial)
-    attn_out = result.astype(jnp.bfloat16).reshape(token_count, -1)
+    groups, head_size = query.shape[2], query.shape[3]
+    req_n = counts.shape[0]
+    width = 2 * head_size
+
+    query = query.reshape(token_count, groups, head_size)
+    query = jnp.concatenate([query, jnp.zeros_like(query)], axis=-1)
+    query = jnp.concatenate([query, jnp.zeros((WIN,) + query.shape[1:], query.dtype)], axis=0)
+    newkv = jnp.concatenate([new_key[:, 0], new_value[:, 0]], axis=-1)
+    newkv = jnp.concatenate([newkv, jnp.zeros((WIN, width), newkv.dtype)], axis=0)
+    q_win = jnp.stack(
+        [lax.dynamic_slice_in_dim(query, starts[j], WIN, 0) for j in range(req_n)]
+    )
+    q_win = jnp.transpose(q_win, (0, 2, 1, 3))
+    nkv_win = jnp.stack(
+        [lax.dynamic_slice_in_dim(newkv, starts[j], WIN, 0) for j in range(req_n)]
+    )
+    out_win = attention(counts, q_win, kv_cache, nkv_win)
+    out_win = jnp.transpose(out_win[..., head_size:], (0, 2, 1, 3)).reshape(
+        req_n, WIN, groups * head_size
+    )
+    result = jnp.zeros((token_count + WIN, groups * head_size), jnp.bfloat16)
+    for j in range(req_n):
+        result = lax.dynamic_update_slice_in_dim(result, out_win[j], starts[j], 0)
+    attn_out = result[:token_count]
+
     partial_value = jnp.dot(
         attn_out, output_weight.reshape(-1, model_width), preferred_element_type=jnp.float32
     )
     per_block = routes.shape[0]
     row_start = lax.axis_index("head") * per_block
-    summed = lax.psum(partial_value.astype(jnp.bfloat16), "head").astype(jnp.float32)
-    attn_rows = lax.dynamic_slice_in_dim(summed, row_start, per_block, 0)
+    attn_rows = lax.psum_scatter(
+        partial_value.astype(jnp.bfloat16), "head", scatter_dimension=0, tiled=True
+    ).astype(jnp.float32)
     base_rows = lax.dynamic_slice_in_dim(whole, row_start, per_block, 0)
     resid = base_rows.astype(jnp.float32) + attn_rows
     moe_in = norm_rows(resid, norm_moe).astype(jnp.bfloat16)

time: 640 us -> 473 us (0.74)
  the two profiles are of different devices: /device:TPU:93 before, /device:TPU:124 now
where the time goes in v1:
time: 473 us; the launch traced here: 471 us
  waiting for transfers between devices  140 us (30%)
  Pallas kernels  82.5 us (17%)
  local copies, waits for them, and re-layouts  81.1 us (17%)
  blocking collectives  77.6 us (16%)
  other arithmetic  33.9 us (7%)
  matrix products  27.1 us (6%)
  between operations  21 us (4%)
  starting transfers between devices  8.47 us (2%)
    all_to_all x1, waiting for transfers between devices, local(): lax.all_to_all(produced, 'req', split_axis=0, concat_axis=0, tiled=True)  110 us
    pallas_call x1, Pallas kernels, attention(): pl.pallas_call(attn_kernel, grid_spec=grid_spec, out_shape=jax.ShapeDtype...  82.5 us
    all_to_all x1, blocking collectives, local(): lax.all_to_all(outgoing, 'req', split_axis=0, concat_axis=0, tiled=True)  77.6 us
    reduce_scatter x1, waiting for transfers between devices, local(): lax.psum_scatter(partial_value.astype(jnp.bfloat16), 'head', scatter_dime...  15.6 us
    gather x1, local copies, waits for them, and re-layouts, local(): outgoing = padded[table].reshape(req_count, per_req, capacity, model_width)  14.3 us
    dynamic_update_slice x4, local copies, waits for them, and re-layouts, local(): result = lax.dynamic_update_slice_in_dim(result, out_win[j], starts[j], 0)  14 us
    all_gather x1, waiting for transfers between devices, local(): whole = lax.all_gather(tokens, 'head', axis=1, tiled=True)  13.5 us
    gather x1, local copies, waits for them, and re-layouts, local(): arrived.reshape(EXPERTS * capacity, model_width)[slot_ids]  10.9 us
  transfers between devices with their start and end apart: 3, of which 3 were waited for; matrix products, arithmetic and copies ran while one was open for 6% of the time, Pallas kernels for 0%

profile of v1, /device:TPU:124, one launch (start us, length us, event | category | flops | bytes accessed | tf_op | source)
XLA Modules:
  0.0 471.5 jit_solution(14798662836277442477)
XLA Ops:
  7.3 1.0 reduce-window.10
  16.1 1.6 fusion.35
  17.7 2.0 copy.69
  19.7 1.0 copy.73
  23.2 13.5 %all-gather.2.cloned.1.call-done = bf16[1024,1536]{0,1:T(8,128)(2,1)} async-done(((bf16[1024,192]{0,1:T(8,128)(2,1)}), bf16[1024,1536]{0,1:T(8,128)(2,1)}) %all-gather.2.cloned.1.call-update) | async-done | bytes 3145744 | tf_op jit(solution)/shard_map/all_gather | solution.py:191
  36.7 2.8 fusion
  39.5 2.1 convolution_bitcast_fusion
  41.6 1.0 fusion.44
  42.6 0.9 constant_dynamic-slice_fusion.3
  43.6 1.7 copy.74
  47.5 3.1 fusion.19
  50.6 0.9 copy-done.3
  52.3 2.6 copy.93
  54.9 2.7 negate_bitcast_fusion
  57.6 1.6 copy.94
  59.2 2.8 copy.70
  62.0 3.1 fusion.17
  65.1 1.0 fusion.27
  66.2 0.9 pad_maximum_fusion.nkv_ref
  67.1 1.3 maximum_bitcast_fusion.q_ref
  68.4 82.5 %shard_map.118 = bf16[4,3,512,128]{3,2,1,0:T(8,128)(2,1)} custom-call(s32[4]{0:T(128)} %bitcast.117, bf16[4,3,512,128]{3,2,1,0:T(8,128)(2,1)} %maximum_bitcast_fusion.q_ref, bf16[4,1,7680,128]{3,2,1,0:T(8,128)(2,1)} %kv_ref.1, bf16[4,512,128]{2,1,0:T(8,128)(2,1)} %pad_maximum_fusion.nkv_ref), custom_call_target="tpu_custom_call" | custom-call | tf_op jit(solution)/shard_map/pallas_call | solution.py:167
  150.9 1.9 slice_bitcast_fusion
  152.8 1.0 fusion.54
  153.8 1.8 copy.78
  155.6 1.8 copy.79
  157.5 1.8 copy.80
  161.0 3.3 dynamic_update_slice.12
  164.3 3.7 dynamic_update_slice.13
  168.0 3.7 dynamic_update_slice.14
  171.7 3.3 dynamic_update_slice.15
  175.0 3.9 convolution_convert_fusion
  179.9 9.0 %reduce-window.11 = s32[32,8,128]{2,1,0:T(8,128)S(1)} reduce-window(s32[32,8,128]{2,1,0:T(8,128)S(1)} %fusion.43, s32[]{:T(128)} %constant.23.clone.1), window={size=1x1x128 pad=0_0x0_0x127_0}, to_apply=%region_7.8 | reduce-window | flops 4161536 | bytes 262148 | tf_op jit(solution)/shard_map/reduce-window.1
  189.6 4.3 scatter_custom_fusion
  194.0 1.8 constant_dynamic-slice_fusion.4
  195.8 1.2 copy.92
  196.9 15.6 %reduce-scatter.2.cloned.1.call-done = bf16[128,1536]{1,0:T(8,128)(2,1)} async-done(((bf16[1024,1536]{1,0:T(8,128)(2,1)}), bf16[128,1536]{1,0:T(8,128)(2,1)}) %reduce-scatter.2.cloned.1.call-update) | async-done | bytes 393232 | tf_op jit(solution)/shard_map/reduce_scatter | solution.py:227
  212.5 1.2 multiply_reduce_fusion
  213.7 1.2 multiply_convert_fusion
  215.7 14.3 %gather_fusion = bf16[2048,1536]{1,0:T(8,128)(2,1)} fusion(bf16[129,1536]{1,0:T(8,128)(2,1)} %concatenate.76, s32[2048]{0:T(1024)S(1)} %fusion.46), kind=kCustom, calls=%fused_computation | custom fusion | bytes 12591104 | tf_op jit(solution)/shard_map/gather | solution.py:246
  230.0 77.6 %all_to_all.10 = bf16[16,2,64,1536]{3,2,1,0:T(8,128)(2,1)S(1)} all-to-all(bf16[16,2,64,1536]{3,2,1,0:T(8,128)(2,1)} %bitcast.98), channel_id=1, replica_groups=mesh['req'=16,'head'=8] {'req'}, dimensions={0} | all-to-all | bytes 12582912 | tf_op jit(solution)/shard_map/all_to_all | solution.py:249
  307.6 10.7 %fusion.8 = f32[16,2,64,1024]{3,2,0,1:T(8,128)} fusion(bf16[2,1536,1024]{2,1,0:T(8,128)(2,1)} %param.22, bf16[16,2,64,1536]{3,2,1,0:T(8,128)(2,1)S(1)} %all_to_all.10), kind=kOutput, calls=%fused_computation.17 | convolution fusion | flops 6442450944 | bytes 20971520 | tf_op jit(solution)/shard_map/sncd,ndf->sncf/dot_general | solution.py:247
  318.4 7.3 %convert_bitcast_fusion = bf16[16,2,64,1536]{3,2,0,1:T(8,128)(2,1)S(1)} fusion(bf16[2,512,1536]{2,1,0:T(8,128)(2,1)S(1)} %copy-done, f32[16,2,64,1024]{3,2,0,1:T(8,128)} %fusion.8), kind=kOutput, calls=%fused_computation.13 | convolution fusion | flops 3230662656 | bytes 17825792 | tf_op jit(solution)/shard_map/sncf,nfd->sncd/dot_general | solution.py:254
  325.7 3.1 copy.88
  328.8 8.4 %all-to-all-start.1 = ((bf16[16,2,64,1536]{3,2,1,0:T(8,128)(2,1)}), bf16[16,2,64,1536]{3,2,1,0:T(8,128)(2,1)}, u32[]{:S(2)}, u32[]{:S(2)}) async-start(bf16[16,2,64,1536]{3,2,1,0:T(8,128)(2,1)} %copy.88), calls=%async_computation.2 | async-start | bytes 12582912 | tf_op jit(solution)/shard_map/all_to_all | solution.py:257
  338.0 110.0 %all-to-all-done.1 = bf16[16,2,64,1536]{3,2,1,0:T(8,128)(2,1)} async-done(((bf16[16,2,64,1536]{3,2,1,0:T(8,128)(2,1)}), bf16[16,2,64,1536]{3,2,1,0:T(8,128)(2,1)}, u32[]{:S(2)}, u32[]{:S(2)}) %all-to-all-start.1) | async-done | bytes 6291488 | tf_op jit(solution)/shard_map/all_to_all | solution.py:257
  448.0 10.9 %gather_fusion.1 = bf16[1024,1536]{1,0:T(8,128)(2,1)} fusion(bf16[2048,1536]{1,0:T(8,128)(2,1)} %bitcast.45, s32[1024]{0:T(1024)S(1)} %broadcast_clamp_fusion), kind=kCustom, calls=%fused_computation.1 | custom fusion | bytes 6295552 | tf_op jit(solution)/shard_map/gather | solution.py:258
  459.0 4.8 %fusion.3 = f32[128,1536]{1,0:T(8,128)S(1)} fusion(bf16[1024,1536]{1,0:T(8,128)(2,1)} %gather_fusion.1, f32[128,8]{1,0:T(8,128)} %copy.89), kind=kLoop, calls=%fused_computation.9 | loop fusion | flops 4521984 | bytes 3936256 | tf_op jit(solution)/shard_map/reduce_sum | solution.py:260
  463.7 0.9 add_convert_fusion
  (64 shorter events, 11.8 us)
Async XLA Ops:
  6.5 311.9 %copy-start = (bf16[2,512,1536]{2,1,0:T(8,128)(2,1)S(1)}, bf16[2,512,1536]{2,1,0:T(8,128)(2,1)}, u32[]{:S(2)}) copy-start(bf16[2,512,1536]{2,1,0:T(8,128)(2,1)} %param.23) | copy-start | bytes 9437188
  6.5 32.9 %copy-start.10 = (f32[1536]{0:T(1024)S(1)}, f32[1536]{0:T(1024)}, u32[]{:S(2)}) copy-start(f32[1536]{0:T(1024)} %param.15) | copy-start | bytes 18436
  6.5 30.1 %all-gather.2.cloned.1.call-start = ((), (), s32[]{:S(2)}) async-start(), calls=%async_computation.3 | async-start | bytes 3538944 | tf_op jit(solution)/shard_map/all_gather | solution.py:191
  7.3 205.2 %reduce-scatter.2.cloned.1.call-start = ((), (), s32[]{:S(2)}) async-start(), calls=%async_computation.4 | async-start | bytes 3538944 | tf_op jit(solution)/shard_map/reduce_scatter | solution.py:227
  36.7 2.8 copy-start.1
  50.6 0.9 copy-start.3
  62.0 4.2 copy-start.4
  62.0 4.2 copy-start.5
  62.0 4.2 copy-start.6
  62.0 4.2 copy-start.7
  178.9 0.7 copy-start.8
  328.8 8.4 %copy-start.9 = (f32[128,8]{0,1:T(8,128)S(1)}, f32[128,8]{0,1:T(8,128)}, u32[]{:S(2)}) copy-start(f32[128,8]{0,1:T(8,128)} %param.21) | copy-start | bytes 12292
  328.8 119.2 %all-to-all-start.1 = ((bf16[16,2,64,1536]{3,2,1,0:T(8,128)(2,1)}), bf16[16,2,64,1536]{3,2,1,0:T(8,128)(2,1)}, u32[]{:S(2)}, u32[]{:S(2)}) async-start(bf16[16,2,64,1536]{3,2,1,0:T(8,128)(2,1)} %copy.88), calls=%async_computation.2 | async-start | bytes 12582912 | tf_op jit(solution)/shard_map/all_to_all | solution.py:257
  459.0 4.8 %copy-start.2 = (bf16[128,1536]{1,0:T(8,128)(2,1)S(1)}, bf16[128,1536]{1,0:T(8,128)(2,1)}, u32[]{:S(2)}) copy-start(bf16[128,1536]{1,0:T(8,128)(2,1)} %reduce-scatter.2.cloned.1.call-done) | copy-start | bytes 1179652
Sparse Core Ops, SparseCore 0:
  9.0 27.5 all-gather.1
  179.0 33.4 reduce-scatter.1

commit v2 on v1

--- a/solution.py
+++ b/solution.py
@@ -67,9 +67,8 @@
     )
     keyval = keyval.reshape(token_count, kv_heads, 2 * head_size)
     cos_part, sin_part = rope_tables(position, head_size)
-    query = rotate(query, cos_part[:, None, None, :], sin_part[:, None, None, :]).astype(
-        jnp.bfloat16
-    )
+    query = rotate(query, cos_part[:, None, None, :], sin_part[:, None, None, :])
+    query = (query * (1.0 / math.sqrt(head_size))).astype(jnp.bfloat16)
     new_key = rotate(keyval[..., :head_size], cos_part[:, None, :], sin_part[:, None, :]).astype(
         jnp.bfloat16
     )
@@ -83,10 +82,10 @@
     kb = pl.program_id(2)
     last = pl.num_programs(2) - 1
     count = counts_ref[j]
+    cached = RATIO * count
     groups, tq, width = q_ref.shape[1], q_ref.shape[2], q_ref.shape[3]
     tk = kv_ref.shape[2]
     win = nkv_ref.shape[1]
-    scale = 1.0 / math.sqrt(width // 2)
     tile_ok = qi * tq < count
 
     @pl.when(kb == 0)
@@ -100,12 +99,13 @@
         s = lax.dot_general(
             q, rows, (((1,), (1,)), ((), ())), preferred_element_type=jnp.float32
         )
-        s = (s * scale).reshape(groups, tq, rows.shape[0])
-        s = jnp.where(mask, s, floor_score)
+        s = s.reshape(groups, tq, rows.shape[0])
+        if mask is not None:
+            s = jnp.where(mask, s, floor_score)
         m_old = m_sc[...]
         m_new = jnp.maximum(m_old, jnp.max(s, axis=-1, keepdims=True))
         alpha = jnp.exp(m_old - m_new)
-        p = jnp.where(mask, jnp.exp(s - m_new), 0.0)
+        p = jnp.exp(s - m_new)
         l_sc[...] = l_sc[...] * alpha + jnp.sum(p, axis=-1, keepdims=True)
         pv = jnp.dot(
             p.astype(jnp.bfloat16).reshape(groups * tq, rows.shape[0]),
@@ -121,10 +121,10 @@
         col = lax.broadcasted_iota(jnp.int32, (1, tq, win), 2)
         absorb(nkv_ref[0], col <= row)
 
-    @pl.when(tile_ok & (kb > 0) & ((kb - 1) * tk < RATIO * count))
+    @pl.when(tile_ok & (kb > 0) & ((kb - 1) * tk < cached))
     def _():
         col = (kb - 1) * tk + lax.broadcasted_iota(jnp.int32, (1, 1, tk), 2)
-        absorb(kv_ref[0, 0], col < RATIO * count)
+        absorb(kv_ref[0, 0], col < cached)
 
     @pl.when(kb == last)
     def _():
@@ -231,19 +231,37 @@
     resid = base_rows.astype(jnp.float32) + attn_rows
     moe_in = norm_rows(resid, norm_moe).astype(jnp.bfloat16)
     capacity = per_block // 2
-    flat_routes = routes.reshape(-1)
     expert_ids = jnp.arange(EXPERTS, dtype=jnp.int32)
-    onehot = (flat_routes[:, None] == expert_ids[None, :]).astype(jnp.int32)
-    before = jnp.cumsum(onehot, axis=0) - onehot
-    rank_in = jnp.sum(before * onehot, axis=1)
-    slot_ids = flat_routes * capacity + rank_in
-    owners = jnp.arange(per_block * TOPK, dtype=jnp.int32) // TOPK
-    table = jnp.full((EXPERTS * capacity,), per_block, jnp.int32).at[slot_ids].set(owners)
-    padded = jnp.concatenate([moe_in, jnp.zeros((1, model_width), jnp.bfloat16)], axis=0)
+    onehot = (routes.reshape(-1)[:, None] == expert_ids[None, :]).astype(jnp.bfloat16)
+    pair_count = onehot.shape[0]
+    chunk = 32
+    lower = (
+        jnp.arange(chunk, dtype=jnp.int32)[:, None] > jnp.arange(chunk, dtype=jnp.int32)[None, :]
+    ).astype(jnp.bfloat16)
+    pieces = onehot.reshape(pair_count // chunk, chunk, EXPERTS)
+    within = jnp.einsum("ij,cje->cie", lower, pieces, preferred_element_type=jnp.float32)
+    piece_total = jnp.sum(pieces.astype(jnp.float32), axis=1)
+    piece_lower = (
+        jnp.arange(pair_count // chunk, dtype=jnp.int32)[:, None]
+        > jnp.arange(pair_count // chunk, dtype=jnp.int32)[None, :]
+    ).astype(jnp.float32)
+    earlier = jnp.dot(piece_lower, piece_total, precision=lax.Precision.HIGHEST)
+    before = (within + earlier[:, None, :]).reshape(pair_count, EXPERTS)
+    rank_in = jnp.sum(before * onehot.astype(jnp.float32), axis=1).astype(jnp.int32)
+    slot_ids = (routes.reshape(-1) * capacity + rank_in).reshape(per_block, TOPK)
+    slot_range = jnp.arange(EXPERTS * capacity, dtype=jnp.int32)
+    hits = slot_ids[:, :, None] == slot_range[None, None, :]
+    send = jnp.any(hits, axis=1).astype(jnp.bfloat16)
+    combine = jnp.sum(jnp.where(hits, route_gain[:, :, None], 0.0), axis=1)
+    combine_hi = combine.astype(jnp.bfloat16)
+    combine_lo = (combine - combine_hi.astype(jnp.float32)).astype(jnp.bfloat16)
     req_count = lax.axis_size("req")
     per_req = w_down.shape[0]
     ff_width = w_down.shape[1]
-    outgoing = padded[table].reshape(req_count, per_req, capacity, model_width)
+    outgoing = lax.dot_general(
+        send, moe_in, (((0,), (0,)), ((), ())), preferred_element_type=jnp.float32
+    ).astype(jnp.bfloat16)
+    outgoing = outgoing.reshape(req_count, per_req, capacity, model_width)
     gate_up = jnp.einsum(
         "sncd,ndf->sncf",
         lax.all_to_all(outgoing, "req", split_axis=0, concat_axis=0, tiled=True),
@@ -255,9 +273,10 @@
         "sncf,nfd->sncd", hidden, w_down, preferred_element_type=jnp.float32
     ).astype(jnp.bfloat16)
     arrived = lax.all_to_all(produced, "req", split_axis=0, concat_axis=0, tiled=True)
-    gathered = arrived.reshape(EXPERTS * capacity, model_width)[slot_ids].astype(jnp.float32)
-    gathered = gathered.reshape(per_block, TOPK, model_width)
-    moe_sum = jnp.sum(gathered * route_gain[..., None], axis=1)
+    arrived = arrived.reshape(EXPERTS * capacity, model_width)
+    moe_sum = jnp.dot(combine_hi, arrived, preferred_element_type=jnp.float32) + jnp.dot(
+        combine_lo, arrived, preferred_element_type=jnp.float32
+    )
     return (resid + moe_sum).astype(jnp.bfloat16)
 
 

time: 473 us -> 447 us (0.945)
  local copies, waits for them, and re-layouts: 81.1 us -> 49.9 us
  matrix products: 27.1 us -> 38.3 us
  other arithmetic: 33.9 us -> 27.4 us
  Pallas kernels: 82.5 us -> 76.1 us
  waiting for transfers between devices: 140 us -> 146 us
    gather x2 -> x0, local copies, waits for them, and re-layouts: 25.3 us -> none  [the longest x1 14.3 us: local(): outgoing = padded[table].reshape(req_count, per_req, capacity, model_width)]
    dot_general x0 -> x5, matrix products: none -> 12.3 us  [the longest x1 4.6 us: local(): jnp.dot(combine_lo, arrived, preferred_element_type=jnp.float32)]
    reduce_scatter x1, waiting for transfers between devices: 15.6 us -> 27.5 us  [local(): lax.psum_scatter(partial_value.astype(jnp.bfloat16), 'head', scatter_dime...]
    another operation x4 -> x1, other arithmetic: 10.1 us -> 0.98 us
    pallas_call x1, Pallas kernels: 82.5 us -> 76.1 us  [attention(): pl.pallas_call(attn_kernel, grid_spec=grid_spec, out_shape=jax.ShapeDtype...]
    all_to_all x1, waiting for transfers between devices: 110 us -> 105 us  [local(): lax.all_to_all(produced, 'req', split_axis=0, concat_axis=0, tiled=True)]
  transfers between devices with their start and end apart: 3 -> 3, of which waited for: 3 -> 3; matrix products, arithmetic and copies ran while one was open for 6% -> 5% of each run, Pallas kernels for 0% -> 0%
where the time goes in v2:
time: 447 us; the launch traced here: 445 us
  waiting for transfers between devices  146 us (33%)
  blocking collectives  77.6 us (17%)
  Pallas kernels  76.1 us (17%)
  local copies, waits for them, and re-layouts  49.9 us (11%)
  matrix products  38.3 us (9%)
  other arithmetic  27.4 us (6%)
  between operations  21.1 us (5%)
  starting transfers between devices  8.53 us (2%)
    all_to_all x1, waiting for transfers between devices, local(): lax.all_to_all(produced, 'req', split_axis=0, concat_axis=0, tiled=True)  105 us
    all_to_all x1, blocking collectives, local(): lax.all_to_all(outgoing, 'req', split_axis=0, concat_axis=0, tiled=True)  77.6 us
    pallas_call x1, Pallas kernels, attention(): pl.pallas_call(attn_kernel, grid_spec=grid_spec, out_shape=jax.ShapeDtype...  76.1 us
    reduce_scatter x1, waiting for transfers between devices, local(): lax.psum_scatter(partial_value.astype(jnp.bfloat16), 'head', scatter_dime...  27.5 us
    dynamic_update_slice x4, local copies, waits for them, and re-layouts, local(): result = lax.dynamic_update_slice_in_dim(result, out_win[j], starts[j], 0)  14.2 us
    all_gather x1, waiting for transfers between devices, local(): whole = lax.all_gather(tokens, 'head', axis=1, tiled=True)  13.3 us
  transfers between devices with their start and end apart: 3, of which 3 were waited for; matrix products, arithmetic and copies ran while one was open for 5% of the time, Pallas kernels for 0%

profile of v2, /device:TPU:124, one launch (start us, length us, event | category | flops | bytes accessed | tf_op | source)
XLA Modules:
  0.0 445.2 jit_solution(9608643660408793473)
XLA Ops:
  7.3 1.0 reduce-window.4
  16.2 1.6 fusion.44
  17.8 2.0 copy.87
  19.8 1.0 copy.91
  23.3 13.3 %all-gather.2.cloned.1.call-done = bf16[1024,1536]{0,1:T(8,128)(2,1)} async-done(((bf16[1024,192]{0,1:T(8,128)(2,1)}), bf16[1024,1536]{0,1:T(8,128)(2,1)}) %all-gather.2.cloned.1.call-update) | async-done | bytes 3145744 | tf_op jit(solution)/shard_map/all_gather | solution.py:191
  36.7 2.6 fusion.1
  39.3 3.0 convolution_bitcast_fusion
  42.3 1.0 fusion.53
  43.3 0.9 constant_dynamic-slice_fusion.3
  44.3 1.7 copy.92
  48.2 3.1 fusion.25
  51.3 0.9 copy-done.3
  53.1 2.6 copy.109
  55.7 2.7 negate_bitcast_fusion
  58.3 1.6 copy.110
  60.0 2.8 copy.88
  62.7 3.2 fusion.20
  66.0 1.0 fusion.34
  67.0 0.9 pad_maximum_fusion.nkv_ref
  67.9 1.3 maximum_bitcast_fusion.q_ref
  69.2 76.1 %shard_map.118 = bf16[4,3,512,128]{3,2,1,0:T(8,128)(2,1)} custom-call(s32[4]{0:T(128)} %bitcast.102, bf16[4,3,512,128]{3,2,1,0:T(8,128)(2,1)} %maximum_bitcast_fusion.q_ref, bf16[4,1,7680,128]{3,2,1,0:T(8,128)(2,1)} %kv_ref.1, bf16[4,512,128]{2,1,0:T(8,128)(2,1)} %pad_maximum_fusion.nkv_ref), custom_call_target="tpu_custom_call" | custom-call | tf_op jit(solution)/shard_map/pallas_call | solution.py:167
  145.3 1.9 slice_bitcast_fusion
  147.2 1.0 fusion.60
  148.3 1.8 copy.96
  150.1 1.8 copy.97
  151.9 1.8 copy.98
  153.8 0.8 copy.99
  154.6 0.9 broadcast_in_dim.10
  155.5 3.3 dynamic_update_slice.12
  158.8 3.7 dynamic_update_slice.13
  162.5 3.7 dynamic_update_slice.14
  166.1 3.5 dynamic_update_slice.15
  169.6 3.9 convolution_convert_fusion.1
  174.7 4.7 %fusion = pred[128,2048]{1,0:T(8,128)(4,1)} fusion(s32[128,8]{1,0:T(8,128)S(1)} %copy.102), kind=kLoop, calls=%fused_computation.2 | loop fusion | flops 3932160 | bytes 266240 | tf_op jit(solution)/shard_map/reduce_or | solution.py:254
  179.3 1.8 constant_dynamic-slice_fusion.4
  181.1 1.2 copy.108
  182.3 27.5 %reduce-scatter.2.cloned.1.call-done = bf16[128,1536]{1,0:T(8,128)(2,1)} async-done(((bf16[1024,1536]{1,0:T(8,128)(2,1)}), bf16[128,1536]{1,0:T(8,128)(2,1)}) %reduce-scatter.2.cloned.1.call-update) | async-done | bytes 393232 | tf_op jit(solution)/shard_map/reduce_scatter | solution.py:227
  209.8 1.2 multiply_reduce_fusion
  211.0 3.1 convolution_convert_fusion
  214.1 77.6 %all_to_all.10 = bf16[16,2,64,1536]{3,2,1,0:T(8,128)(2,1)S(1)} all-to-all(bf16[16,2,64,1536]{3,2,1,0:T(8,128)(2,1)S(1)} %bitcast.88), channel_id=1, replica_groups=mesh['req'=16,'head'=8] {'req'}, dimensions={0} | all-to-all | bytes 12582912 | tf_op jit(solution)/shard_map/all_to_all | solution.py:267
  291.7 8.8 %fusion.8 = f32[16,2,64,1024]{3,2,0,1:T(8,128)} fusion(bf16[2,1536,1024]{2,1,0:T(8,128)(2,1)S(1)} %bitcast.105, bf16[16,2,64,1536]{3,2,1,0:T(8,128)(2,1)S(1)} %all_to_all.10), kind=kOutput, calls=%fused_computation.16 | convolution fusion | flops 6442450944 | bytes 20971520 | tf_op jit(solution)/shard_map/sncd,ndf->sncf/dot_general | solution.py:265
  300.5 7.3 %convert_bitcast_fusion = bf16[16,2,64,1536]{3,2,0,1:T(8,128)(2,1)S(1)} fusion(bf16[2,512,1536]{2,1,0:T(8,128)(2,1)S(1)} %copy-done, f32[16,2,64,1024]{3,2,0,1:T(8,128)} %fusion.8), kind=kOutput, calls=%fused_computation.12 | convolution fusion | flops 3230662656 | bytes 17825792 | tf_op jit(solution)/shard_map/sncf,nfd->sncd/dot_general | solution.py:272
  307.8 3.2 copy.105
  310.9 8.5 %all-to-all-start.1 = ((bf16[16,2,64,1536]{3,2,1,0:T(8,128)(2,1)}), bf16[16,2,64,1536]{3,2,1,0:T(8,128)(2,1)}, u32[]{:S(2)}, u32[]{:S(2)}) async-start(bf16[16,2,64,1536]{3,2,1,0:T(8,128)(2,1)} %copy.105), calls=%async_computation.2 | async-start | bytes 12582912 | tf_op jit(solution)/shard_map/all_to_all | solution.py:275
  320.2 4.7 %select_reduce_fusion = f32[128,2048]{1,0:T(8,128)} fusion(f32[128,8]{1,0:T(8,128)} %copy.103, s32[128,8]{1,0:T(8,128)} %copy-done.4), kind=kLoop, calls=%fused_computation | loop fusion | flops 6029312 | bytes 1056768 | tf_op jit(solution)/shard_map/reduce_sum | solution.py:255
  324.8 104.7 %all-to-all-done.1 = bf16[16,2,64,1536]{3,2,1,0:T(8,128)(2,1)} async-done(((bf16[16,2,64,1536]{3,2,1,0:T(8,128)(2,1)}), bf16[16,2,64,1536]{3,2,1,0:T(8,128)(2,1)}, u32[]{:S(2)}, u32[]{:S(2)}) %all-to-all-start.1) | async-done | bytes 6291488 | tf_op jit(solution)/shard_map/all_to_all | solution.py:275
  429.5 4.2 fusion.49
  433.7 4.6 %fusion.15 = bf16[128,1536]{1,0:T(8,128)(2,1)} fusion(f32[128,1536]{1,0:T(8,128)S(1)} %fusion.49, bf16[2048,1536]{1,0:T(8,128)(2,1)} %bitcast.43, bf16[128,1536]{1,0:T(8,128)(2,1)S(1)} %copy-done.2, bf16[128,1536]{1,0:T(8,128)(2,1)S(1)} %copy.108, f32[128,2048]{1,0:T(8,128)S(1)} %copy-done.1), kind=kOutput, calls=%fused_computation.20 | convolution fusion | flops 807534592 | bytes 9306112 | tf_op jit(solution)/shard_map/dot_general | solution.py:277
  (62 shorter events, 8.7 us)
Async XLA Ops:
  6.5 294.0 %copy-start = (bf16[2,512,1536]{2,1,0:T(8,128)(2,1)S(1)}, bf16[2,512,1536]{2,1,0:T(8,128)(2,1)}, u32[]{:S(2)}) copy-start(bf16[2,512,1536]{2,1,0:T(8,128)(2,1)} %param.23) | copy-start | bytes 9437188
  6.5 32.7 %copy-start.12 = (f32[1536]{0:T(1024)S(1)}, f32[1536]{0:T(1024)}, u32[]{:S(2)}) copy-start(f32[1536]{0:T(1024)} %param.15) | copy-start | bytes 18436
  6.5 30.1 %all-gather.2.cloned.1.call-start = ((), (), s32[]{:S(2)}) async-start(), calls=%async_computation.3 | async-start | bytes 3538944 | tf_op jit(solution)/shard_map/all_gather | solution.py:191
  7.3 202.5 %reduce-scatter.2.cloned.1.call-start = ((), (), s32[]{:S(2)}) async-start(), calls=%async_computation.4 | async-start | bytes 3538944 | tf_op jit(solution)/shard_map/reduce_scatter | solution.py:227
  51.3 1.0 copy-start.3
  62.7 4.2 copy-start.5
  62.7 4.3 copy-start.6
  62.7 4.3 copy-start.7
  62.7 4.3 copy-start.8
  169.6 3.9 copy-start.9
  173.5 37.5 %copy-start.10 = (f32[1536]{0:T(1024)S(1)}, f32[1536]{0:T(1024)}, u32[]{:S(2)}) copy-start(f32[1536]{0:T(1024)} %param.19) | copy-start | bytes 18436
  174.7 4.7 %copy-start.4 = (s32[128,8]{1,0:T(8,128)}, s32[128,8]{1,0:T(8,128)S(1)}, u32[]{:S(2)}) copy-start(s32[128,8]{1,0:T(8,128)S(1)} %copy.102) | copy-start | bytes 12292
  211.0 80.7 %slice-start = ((s8[6291456]{0:T(1024)(128)(4,1)}), s8[4194304]{0:T(1024)(128)(4,1)S(1)}, s32[]{:S(2)}) async-start(s8[6291456]{0:T(1024)(128)(4,1)} %bitcast.104), calls=%async_computation.5 | async-start | bytes 8388608
  214.1 77.6 %slice-start.1 = ((s8[6291456]{0:T(1024)(128)(4,1)}), s8[2097152]{0:T(1024)(128)(4,1)S(1)}, s32[]{:S(2)}) async-start(s8[6291456]{0:T(1024)(128)(4,1)} %bitcast.104), calls=%async_computation.6 | async-start | bytes 4194304
  310.9 8.5 %copy-start.11 = (f32[128,8]{0,1:T(8,128)S(1)}, f32[128,8]{0,1:T(8,128)}, u32[]{:S(2)}) copy-start(f32[128,8]{0,1:T(8,128)} %param.21) | copy-start | bytes 12292
  310.9 118.6 %all-to-all-start.1 = ((bf16[16,2,64,1536]{3,2,1,0:T(8,128)(2,1)}), bf16[16,2,64,1536]{3,2,1,0:T(8,128)(2,1)}, u32[]{:S(2)}, u32[]{:S(2)}) async-start(bf16[16,2,64,1536]{3,2,1,0:T(8,128)(2,1)} %copy.105), calls=%async_computation.2 | async-start | bytes 12582912 | tf_op jit(solution)/shard_map/all_to_all | solution.py:275
  429.5 4.2 copy-start.1
  429.5 4.2 copy-start.2
Sparse Core Ops, SparseCore 0:
  9.0 27.5 all-gather.1
  173.7 36.0 reduce-scatter.1

commit v3 on v2

--- a/solution.py
+++ b/solution.py
@@ -83,7 +83,7 @@
     last = pl.num_programs(2) - 1
     count = counts_ref[j]
     cached = RATIO * count
-    groups, tq, width = q_ref.shape[1], q_ref.shape[2], q_ref.shape[3]
+    groups, tq, width = q_ref.shape[0], q_ref.shape[2], q_ref.shape[3]
     tk = kv_ref.shape[2]
     win = nkv_ref.shape[1]
     tile_ok = qi * tq < count
@@ -95,7 +95,7 @@
         acc_sc[...] = jnp.zeros(acc_sc.shape, jnp.float32)
 
     def absorb(rows, mask):
-        q = q_ref[0].reshape(groups * tq, width)
+        q = q_ref[:, 0].reshape(groups * tq, width)
         s = lax.dot_general(
             q, rows, (((1,), (1,)), ((), ())), preferred_element_type=jnp.float32
         )
@@ -130,18 +130,18 @@
     def _():
         total = l_sc[...]
         total = jnp.where(total > 0.0, total, 1.0)
-        o_ref[0] = (acc_sc[...] / total).astype(o_ref.dtype)
+        o_ref[:, 0] = (acc_sc[...] / total).astype(o_ref.dtype)
 
 
 def attention(counts, q_win, kv_cache, nkv_win):
-    req_n, groups, win, width = q_win.shape
+    groups, req_n, win, width = q_win.shape
     cache_len = kv_cache.shape[2]
     n_tiles = win // TQ
     n_blocks = cache_len // TK
 
     def q_map(j, qi, kb, cnt):
         tiles = (cnt[j] + TQ - 1) // TQ
-        return (j, 0, jnp.minimum(qi, tiles - 1), 0)
+        return (0, j, jnp.minimum(qi, tiles - 1), 0)
 
     def kv_map(j, qi, kb, cnt):
         tiles = (cnt[j] + TQ - 1) // TQ
@@ -153,11 +153,11 @@
         num_scalar_prefetch=1,
         grid=(req_n, n_tiles, n_blocks + 1),
         in_specs=[
-            pl.BlockSpec((1, groups, TQ, width), q_map),
+            pl.BlockSpec((groups, 1, TQ, width), q_map),
             pl.BlockSpec((1, 1, TK, width), kv_map),
             pl.BlockSpec((1, win, width), lambda j, qi, kb, cnt: (j, 0, 0)),
         ],
-        out_specs=pl.BlockSpec((1, groups, TQ, width), lambda j, qi, kb, cnt: (j, 0, qi, 0)),
+        out_specs=pl.BlockSpec((groups, 1, TQ, width), lambda j, qi, kb, cnt: (0, j, qi, 0)),
         scratch_shapes=[
             pltpu.VMEM((groups, TQ, 1), jnp.float32),
             pltpu.VMEM((groups, TQ, 1), jnp.float32),
@@ -172,6 +172,11 @@
             dimension_semantics=("arbitrary", "arbitrary", "arbitrary")
         ),
     )(counts, q_win, kv_cache, nkv_win)
+
+
+def turned_columns(weight):
+    half = weight.shape[-1] // 2
+    return jnp.concatenate([-weight[..., half:], weight[..., :half]], axis=-1)
 
 
 def local(
@@ -193,42 +198,63 @@
     normed = norm_rows(whole.astype(jnp.float32), norm_attn).astype(jnp.bfloat16)
     counts = new_counts[0]
     starts, position = request_layout(counts, token_count, RATIO)
-    query, new_key, new_value = project(normed, query_weight, key_value_weight, position)
-    groups, head_size = query.shape[2], query.shape[3]
     req_n = counts.shape[0]
+    head_size = key_value_weight.shape[2] // 2
+    groups = query_weight.shape[2] // head_size
     width = 2 * head_size
 
-    query = query.reshape(token_count, groups, head_size)
-    query = jnp.concatenate([query, jnp.zeros_like(query)], axis=-1)
-    query = jnp.concatenate([query, jnp.zeros((WIN,) + query.shape[1:], query.dtype)], axis=0)
-    newkv = jnp.concatenate([new_key[:, 0], new_value[:, 0]], axis=-1)
-    newkv = jnp.concatenate([newkv, jnp.zeros((WIN, width), newkv.dtype)], axis=0)
-    q_win = jnp.stack(
-        [lax.dynamic_slice_in_dim(query, starts[j], WIN, 0) for j in range(req_n)]
-    )
-    q_win = jnp.transpose(q_win, (0, 2, 1, 3))
-    nkv_win = jnp.stack(
-        [lax.dynamic_slice_in_dim(newkv, starts[j], WIN, 0) for j in range(req_n)]
-    )
+    cos_part, sin_part = rope_tables(position, head_size)
+    scale = 1.0 / math.sqrt(head_size)
+    no_lanes = jnp.zeros((token_count, width - head_size), jnp.float32)
+    cos_q = jnp.concatenate([cos_part * scale, no_lanes], axis=1)
+    sin_q = jnp.concatenate([sin_part * scale, no_lanes], axis=1)
+    q_weight = query_weight.reshape(model_width, groups, head_size)
+    no_cols = jnp.zeros((model_width, groups, width - head_size), q_weight.dtype)
+    q_plain = jnp.concatenate([q_weight, no_cols], axis=-1)
+    q_turned = jnp.concatenate([turned_columns(q_weight), no_cols], axis=-1)
+    q_a = jnp.einsum("td,dgc->gtc", normed, q_plain, preferred_element_type=jnp.float32)
+    q_b = jnp.einsum("td,dgc->gtc", normed, q_turned, preferred_element_type=jnp.float32)
+    query = (q_a * cos_q[None] + q_b * sin_q[None]).astype(jnp.bfloat16)
+
+    kv_weight = key_value_weight.reshape(model_width, width)
+    k_turned = jnp.concatenate(
+        [turned_columns(kv_weight[:, :head_size]), jnp.zeros_like(kv_weight[:, head_size:])],
+        axis=1,
+    )
+    ones_lanes = jnp.ones((token_count, width - head_size), jnp.float32)
+    cos_k = jnp.concatenate([cos_part, ones_lanes], axis=1)
+    sin_k = jnp.concatenate([sin_part, no_lanes], axis=1)
+    kv_a = jnp.dot(normed, kv_weight, preferred_element_type=jnp.float32)
+    kv_b = jnp.dot(normed, k_turned, preferred_element_type=jnp.float32)
+    newkv = (kv_a * cos_k + kv_b * sin_k).astype(jnp.bfloat16)
+
+    row_ids = jnp.arange(token_count, dtype=jnp.int32)
+    offsets = jnp.arange(WIN, dtype=jnp.int32)
+    select = (row_ids[:, None, None] == starts[None, :, None] + offsets[None, None, :]) & (
+        offsets[None, None, :] < counts[None, :, None]
+    )
+    select = select.astype(jnp.bfloat16).reshape(token_count, req_n * WIN)
+    q_win = jnp.einsum("tw,gtc->gwc", select, query, preferred_element_type=jnp.float32)
+    q_win = q_win.astype(jnp.bfloat16).reshape(groups, req_n, WIN, width)
+    nkv_win = jnp.einsum("tw,tc->wc", select, newkv, preferred_element_type=jnp.float32)
+    nkv_win = nkv_win.astype(jnp.bfloat16).reshape(req_n, WIN, width)
     out_win = attention(counts, q_win, kv_cache, nkv_win)
-    out_win = jnp.transpose(out_win[..., head_size:], (0, 2, 1, 3)).reshape(
-        req_n, WIN, groups * head_size
-    )
-    result = jnp.zeros((token_count + WIN, groups * head_size), jnp.bfloat16)
-    for j in range(req_n):
-        result = lax.dynamic_update_slice_in_dim(result, out_win[j], starts[j], 0)
-    attn_out = result[:token_count]
-
-    partial_value = jnp.dot(
-        attn_out, output_weight.reshape(-1, model_width), preferred_element_type=jnp.float32
+    out_win = out_win.reshape(groups, req_n * WIN, width)
+    attn_rows = jnp.einsum("tw,gwc->gtc", select, out_win, preferred_element_type=jnp.float32)
+    attn_rows = attn_rows.astype(jnp.bfloat16)
+    o_weight = output_weight.reshape(groups, head_size, model_width)
+    o_weight = jnp.concatenate([jnp.zeros_like(o_weight), o_weight], axis=1)
+
+    partial_value = jnp.einsum(
+        "gtc,gcd->td", attn_rows, o_weight, preferred_element_type=jnp.float32
     )
     per_block = routes.shape[0]
     row_start = lax.axis_index("head") * per_block
-    attn_rows = lax.psum_scatter(
+    summed = lax.psum_scatter(
         partial_value.astype(jnp.bfloat16), "head", scatter_dimension=0, tiled=True
     ).astype(jnp.float32)
     base_rows = lax.dynamic_slice_in_dim(whole, row_start, per_block, 0)
-    resid = base_rows.astype(jnp.float32) + attn_rows
+    resid = base_rows.astype(jnp.float32) + summed
     moe_in = norm_rows(resid, norm_moe).astype(jnp.bfloat16)
     capacity = per_block // 2
     expert_ids = jnp.arange(EXPERTS, dtype=jnp.int32)

time: 447 us -> 422 us (0.944)
  local copies, waits for them, and re-layouts: 49.9 us -> 18.9 us
  matrix products: 38.3 us -> 57.7 us
  between operations: 21.1 us -> 13.6 us
    dot_general x3 -> x5, matrix products: 9.95 us -> 29.4 us  [the longest x1 7.41 us: local(): jnp.einsum('tw,gtc->gwc', select, query, preferred_element_type=jnp.float32)]
    dynamic_update_slice x4 -> x0, local copies, waits for them, and re-layouts: 14.2 us -> none  [local(): result = lax.dynamic_update_slice_in_dim(result, out_win[j], starts[j], 0)]
    slice x7 -> x0, local copies, waits for them, and re-layouts: 8.81 us -> none  [the longest x5 7.35 us: local(): result = lax.dynamic_update_slice_in_dim(result, out_win[j], starts[j], 0)]
    dynamic_slice x5 -> x0, local copies, waits for them, and re-layouts: 4.87 us -> none  [local(): lax.dynamic_slice_in_dim(newkv, starts[j], WIN, 0)]
  transfers between devices with their start and end apart: 3 -> 3, of which waited for: 3 -> 3; matrix products, arithmetic and copies ran while one was open for 5% -> 8% of each run, Pallas kernels for 0% -> 0%
where the time goes in v3:
time: 422 us; the launch traced here: 420 us
  waiting for transfers between devices  143 us (34%)
  blocking collectives  77.9 us (18%)
  Pallas kernels  77 us (18%)
  matrix products  57.7 us (14%)
  other arithmetic  23.8 us (6%)
  local copies, waits for them, and re-layouts  18.9 us (4%)
  between operations  13.6 us (3%)
  starting transfers between devices  8.33 us (2%)
    all_to_all x1, waiting for transfers between devices, local(): lax.all_to_all(produced, 'req', split_axis=0, concat_axis=0, tiled=True)  107 us
    all_to_all x1, blocking collectives, local(): lax.all_to_all(outgoing, 'req', split_axis=0, concat_axis=0, tiled=True)  77.9 us
    pallas_call x1, Pallas kernels, attention(): pl.pallas_call(attn_kernel, grid_spec=grid_spec, out_shape=jax.ShapeDtype...  77 us
    reduce_scatter x1, waiting for transfers between devices, local(): lax.psum_scatter(partial_value.astype(jnp.bfloat16), 'head', scatter_dime...  24.1 us
    all_gather x1, waiting for transfers between devices, local(): whole = lax.all_gather(tokens, 'head', axis=1, tiled=True)  10.9 us
    dot_general x1, matrix products, local(): jnp.einsum('sncd,ndf->sncf', lax.all_to_all(outgoing, 'req', split_axis=0...  8.82 us
  transfers between devices with their start and end apart: 3, of which 3 were waited for; matrix products, arithmetic and copies ran while one was open for 8% of the time, Pallas kernels for 0%

profile of v3, /device:TPU:124, one launch (start us, length us, event | category | flops | bytes accessed | tf_op | source)
XLA Modules:
  0.0 420.2 jit_solution(9479009435331752258)
XLA Ops:
  6.5 0.7 all-gather.2.cloned.1.call-update
  7.3 1.0 reduce-window.4
  8.3 0.1 convert_reduce_fusion.1
  8.4 0.7 fusion.92
  9.1 0.8 select_reduce_fusion.2
  9.8 0.2 broadcast_multiply_fusion.2
  10.1 3.2 fusion.77
  13.3 1.9 copy.82
  15.2 1.9 copy.83
  17.1 1.8 concatenate.29.clone
  18.9 1.8 concatenate.31.clone
  20.9 0.6 pad.11.clone
  21.6 0.7 iota_compare_fusion.9
  22.2 0.7 iota_add_fusion
  22.9 1.9 slice_negate_fusion.1
  24.8 1.0 slice_negate_fusion
  25.8 10.9 %all-gather.2.cloned.1.call-done = bf16[1024,1536]{0,1:T(8,128)(2,1)} async-done(((bf16[1024,192]{0,1:T(8,128)(2,1)}), bf16[1024,1536]{0,1:T(8,128)(2,1)}) %all-gather.2.cloned.1.call-update) | async-done | bytes 3145744 | tf_op jit(solution)/shard_map/all_gather | solution.py:196
  36.7 2.8 fusion.11
  39.5 3.7 fusion.30
  43.3 7.4 %fusion.37 = bf16[3,2048,128]{1,2,0:T(8,128)(2,1)} fusion(s32[2048]{0:T(1024)S(1)} %add.125, pred[2048]{0:T(1024)(128)(4,1)S(1)} %lt.29, f32[3,128,1024]{2,1,0:T(8,128)} %fusion.30, bf16[1536,3,64]{0,2,1:T(8,128)(2,1)} %bitcast.115, f32[1024,128]{0,1:T(8,128)} %concatenate.31.clone, f32[1024,128]{0,1:T(8,128)} %concatenate.29.clone, ...), kind=kOutput, calls=%fused_computation.38 | convolution fusion | flops 2831417344 | bytes 7950336 | tf_op jit(solution)/shard_map/tw,gtc->gwc/dot_general | solution.py:237
  50.7 2.6 copy.63
  53.3 4.6 %convolution_multiply_fusion = f32[1024,128]{1,0:T(8,128)} fusion(f32[1024,64]{1,0:T(8,128)} %get-tuple-element.12, bf16[1536,32]{1,0:T(8,128)(2,1)} %get-tuple-element.14, bf16[1536,32]{1,0:T(8,128)(2,1)} %get-tuple-element.13, bf16[128]{0:T(256)(128)(2,1)} %pad.11.clone, bf16[1024,1536]{0,1:T(8,128)(2,1)} %all-gather.2.cloned.1.call-done, ...), kind=kOutput, calls=%fused_computation.50 | convolution fusion | flops 410255360 | bytes 4139264 | tf_op jit(solution)/shard_map/dot_general | solution.py:228
  57.9 6.7 %fusion.42 = bf16[2048,128]{1,0:T(8,128)(2,1)} fusion(s32[2048]{0:T(1024)S(1)} %add.125, pred[2048]{0:T(1024)(128)(4,1)S(1)} %lt.29, f32[1024,128]{1,0:T(8,128)} %convolution_multiply_fusion, f32[1024,64]{1,0:T(8,128)} %get-tuple-element.9, bf16[1536,1,128]{2,0,1:T(8,128)(2,1)S(1)} %copy-done.4, bf16[1024,1536]{0,1:T(8,128)(2,1)} %all-gather.2.cloned.1.call-done, ...), kind=kOutput, calls=%fused_computation.42 | convolution fusion | flops 950665216 | bytes 4870144 | tf_op jit(solution)/shard_map/tw,tc->wc/dot_general | solution.py:239
  64.6 77.0 %shard_map.118 = bf16[3,4,512,128]{3,2,1,0:T(8,128)(2,1)} custom-call(s32[4]{0:T(128)} %bitcast.123, bf16[3,4,512,128]{3,2,1,0:T(8,128)(2,1)} %bitcast.112, bf16[4,1,7680,128]{3,2,1,0:T(8,128)(2,1)} %kv_ref.1, bf16[4,512,128]{2,1,0:T(8,128)(2,1)} %bitcast.116), custom_call_target="tpu_custom_call" | custom-call | tf_op jit(solution)/shard_map/pallas_call | solution.py:167
  141.6 6.9 %bitcast_convert_fusion = bf16[1024,1536]{1,0:T(8,128)(2,1)} fusion(bf16[3,64,1536]{2,1,0:T(8,128)(2,1)} %bitcast.129, bf16[3,4,512,128]{3,2,1,0:T(8,128)(2,1)} %shard_map.118, s32[4,512]{1,0:T(4,128)S(1)} %copy-done.9, pred[4,512]{1,0:T(4,128)(4,1)S(1)} %copy-done.11), kind=kOutput, calls=%fused_computation.20 | convolution fusion | flops 2824732672 | bytes 5318656 | tf_op jit(solution)/shard_map/gtc,gcd->td/dot_general | solution.py:248
  148.6 0.7 copy-done.6
  149.2 0.1 copy.66
  149.3 0.1 eq.73
  149.4 0.2 convert_reduce_fusion
  149.6 0.1 fusion.89
  149.7 0.3 fusion.66
  150.2 0.1 copy.68
  150.3 4.7 %fusion = pred[128,2048]{1,0:T(8,128)(4,1)} fusion(s32[128,8]{1,0:T(8,128)S(1)} %copy.68), kind=kLoop, calls=%fused_computation.2 | loop fusion | flops 3932160 | bytes 266240 | tf_op jit(solution)/shard_map/reduce_or | solution.py:280
  155.0 1.8 constant_dynamic-slice_fusion
  156.8 1.2 copy.81
  157.9 24.1 %reduce-scatter.2.cloned.1.call-done = bf16[128,1536]{1,0:T(8,128)(2,1)} async-done(((bf16[1024,1536]{1,0:T(8,128)(2,1)}), bf16[128,1536]{1,0:T(8,128)(2,1)}) %reduce-scatter.2.cloned.1.call-update) | async-done | bytes 393232 | tf_op jit(solution)/shard_map/reduce_scatter | solution.py:253
  182.1 1.2 multiply_reduce_fusion
  183.3 3.1 convolution_convert_fusion
  186.4 77.9 %all_to_all.10 = bf16[16,2,64,1536]{3,2,1,0:T(8,128)(2,1)S(1)} all-to-all(bf16[16,2,64,1536]{3,2,1,0:T(8,128)(2,1)S(1)} %bitcast.111), channel_id=1, replica_groups=mesh['req'=16,'head'=8] {'req'}, dimensions={0} | all-to-all | bytes 12582912 | tf_op jit(solution)/shard_map/all_to_all | solution.py:293
  264.3 8.8 %fusion.24 = f32[16,2,64,1024]{3,2,0,1:T(8,128)} fusion(bf16[2,1536,1024]{2,1,0:T(8,128)(2,1)S(1)} %bitcast.128, bf16[16,2,64,1536]{3,2,1,0:T(8,128)(2,1)S(1)} %all_to_all.10), kind=kOutput, calls=%fused_computation.31 | convolution fusion | flops 6442450944 | bytes 20971520 | tf_op jit(solution)/shard_map/sncd,ndf->sncf/dot_general | solution.py:291
  273.1 7.3 %convert_bitcast_fusion = bf16[16,2,64,1536]{3,2,0,1:T(8,128)(2,1)S(1)} fusion(bf16[2,512,1536]{2,1,0:T(8,128)(2,1)S(1)} %copy-done, f32[16,2,64,1024]{3,2,0,1:T(8,128)} %fusion.24), kind=kOutput, calls=%fused_computation.22 | convolution fusion | flops 3230662656 | bytes 17825792 | tf_op jit(solution)/shard_map/sncf,nfd->sncd/dot_general | solution.py:298
  280.4 3.1 copy.71
  283.6 8.3 %all-to-all-start.1 = ((bf16[16,2,64,1536]{3,2,1,0:T(8,128)(2,1)}), bf16[16,2,64,1536]{3,2,1,0:T(8,128)(2,1)}, u32[]{:S(2)}, u32[]{:S(2)}) async-start(bf16[16,2,64,1536]{3,2,1,0:T(8,128)(2,1)} %copy.71), calls=%async_computation.2 | async-start | bytes 12582912 | tf_op jit(solution)/shard_map/all_to_all | solution.py:301
  291.9 0.7 copy.69
  292.6 4.7 %select_reduce_fusion = f32[128,2048]{1,0:T(8,128)} fusion(f32[128,8]{1,0:T(8,128)} %copy.69, s32[128,8]{1,0:T(8,128)} %copy-done.5), kind=kLoop, calls=%fused_computation | loop fusion | flops 6029312 | bytes 1056768 | tf_op jit(solution)/shard_map/reduce_sum | solution.py:281
  297.3 107.3 %all-to-all-done.1 = bf16[16,2,64,1536]{3,2,1,0:T(8,128)(2,1)} async-done(((bf16[16,2,64,1536]{3,2,1,0:T(8,128)(2,1)}), bf16[16,2,64,1536]{3,2,1,0:T(8,128)(2,1)}, u32[]{:S(2)}, u32[]{:S(2)}) %all-to-all-start.1) | async-done | bytes 6291488 | tf_op jit(solution)/shard_map/all_to_all | solution.py:301
  404.6 4.2 fusion.85
  408.8 4.6 %fusion.41 = bf16[128,1536]{1,0:T(8,128)(2,1)} fusion(f32[128,1536]{1,0:T(8,128)S(1)} %fusion.85, bf16[2048,1536]{1,0:T(8,128)(2,1)} %bitcast.32, bf16[128,1536]{1,0:T(8,128)(2,1)S(1)} %copy-done.3, bf16[128,1536]{1,0:T(8,128)(2,1)S(1)} %copy.81, f32[128,2048]{1,0:T(8,128)S(1)} %copy-done.1), kind=kOutput, calls=%fused_computation.41 | convolution fusion | flops 807534592 | bytes 9306112 | tf_op jit(solution)/shard_map/dot_general | solution.py:303
  (51 shorter events, 0.5 us)
Async XLA Ops:
  6.5 266.6 %copy-start = (bf16[2,512,1536]{2,1,0:T(8,128)(2,1)S(1)}, bf16[2,512,1536]{2,1,0:T(8,128)(2,1)}, u32[]{:S(2)}) copy-start(bf16[2,512,1536]{2,1,0:T(8,128)(2,1)} %param.23) | copy-start | bytes 9437188
  6.5 30.2 %all-gather.2.cloned.1.call-start = ((), (), s32[]{:S(2)}) async-start(), calls=%async_computation.3 | async-start | bytes 3538944 | tf_op jit(solution)/shard_map/all_gather | solution.py:196
  7.3 174.8 %reduce-scatter.2.cloned.1.call-start = ((), (), s32[]{:S(2)}) async-start(), calls=%async_computation.4 | async-start | bytes 3538944 | tf_op jit(solution)/shard_map/reduce_scatter | solution.py:253
  9.8 10.9 %copy-start.8 = (s32[1,4]{1,0:T(1,128)S(1)}, s32[1,4]{1,0:T(1,128)}, u32[]{:S(2)}) copy-start(s32[1,4]{1,0:T(1,128)} %param.13) | copy-start | bytes 52
  10.0 14.8 %copy-start.4 = (bf16[1536,1,128]{2,0,1:T(8,128)(2,1)S(1)}, bf16[1536,1,128]{2,0,1:T(8,128)(2,1)}, u32[]{:S(2)}) copy-start(bf16[1536,1,128]{2,0,1:T(8,128)(2,1)} %param.17) | copy-start | bytes 1179652
  36.7 2.8 copy-start.2
  36.7 2.8 copy-start.12
  36.7 2.8 copy-start.13
  64.6 77.0 %copy-start.9 = (s32[4,512]{1,0:T(4,128)S(1)}, s32[4,512]{1,0:T(4,128)}, u32[]{:S(2)}) copy-start(s32[4,512]{1,0:T(4,128)} %iota_add_fusion) | copy-start | bytes 24580
  64.6 77.0 %copy-start.11 = (pred[4,512]{1,0:T(4,128)(4,1)S(1)}, pred[4,512]{1,0:T(4,128)(4,1)}, u32[]{:S(2)}) copy-start(pred[4,512]{1,0:T(4,128)(4,1)} %iota_compare_fusion.9) | copy-start | bytes 6148
  148.5 0.7 copy-start.6
  148.5 34.7 %copy-start.7 = (f32[1536]{0:T(1024)S(1)}, f32[1536]{0:T(1024)}, u32[]{:S(2)}) copy-start(f32[1536]{0:T(1024)} %param.19) | copy-start | bytes 18436
  150.3 4.7 %copy-start.5 = (s32[128,8]{1,0:T(8,128)}, s32[128,8]{1,0:T(8,128)S(1)}, u32[]{:S(2)}) copy-start(s32[128,8]{1,0:T(8,128)S(1)} %copy.68) | copy-start | bytes 12292
  183.3 81.0 %slice-start = ((s8[6291456]{0:T(1024)(128)(4,1)}), s8[4194304]{0:T(1024)(128)(4,1)S(1)}, s32[]{:S(2)}) async-start(s8[6291456]{0:T(1024)(128)(4,1)} %bitcast.127), calls=%async_computation.5 | async-start | bytes 8388608
  186.4 77.9 %slice-start.1 = ((s8[6291456]{0:T(1024)(128)(4,1)}), s8[2097152]{0:T(1024)(128)(4,1)S(1)}, s32[]{:S(2)}) async-start(s8[6291456]{0:T(1024)(128)(4,1)} %bitcast.127), calls=%async_computation.6 | async-start | bytes 4194304
  283.6 8.3 %copy-start.10 = (f32[128,8]{0,1:T(8,128)S(1)}, f32[128,8]{0,1:T(8,128)}, u32[]{:S(2)}) copy-start(f32[128,8]{0,1:T(8,128)} %param.21) | copy-start | bytes 12292
  283.6 121.0 %all-to-all-start.1 = ((bf16[16,2,64,1536]{3,2,1,0:T(8,128)(2,1)}), bf16[16,2,64,1536]{3,2,1,0:T(8,128)(2,1)}, u32[]{:S(2)}, u32[]{:S(2)}) async-start(bf16[16,2,64,1536]{3,2,1,0:T(8,128)(2,1)} %copy.71), calls=%async_computation.2 | async-start | bytes 12582912 | tf_op jit(solution)/shard_map/all_to_all | solution.py:301
  404.6 4.2 %copy-start.1 = (f32[128,2048]{1,0:T(8,128)S(1)}, f32[128,2048]{1,0:T(8,128)}, u32[]{:S(2)}) copy-start(f32[128,2048]{1,0:T(8,128)} %select_reduce_fusion) | copy-start | bytes 3145732
  404.6 4.2 %copy-start.3 = (bf16[128,1536]{1,0:T(8,128)(2,1)S(1)}, bf16[128,1536]{1,0:T(8,128)(2,1)}, u32[]{:S(2)}) copy-start(bf16[128,1536]{1,0:T(8,128)(2,1)} %reduce-scatter.2.cloned.1.call-done) | copy-start | bytes 1179652
Sparse Core Ops, SparseCore 0:
  9.0 27.6 all-gather.1
  148.7 33.3 reduce-scatter.1

commit v4 on v3

--- a/solution.py
+++ b/solution.py
@@ -194,6 +194,7 @@
     w_down,
 ):
     whole = lax.all_gather(tokens, "head", axis=1, tiled=True)
+    o_weight_all = lax.all_gather(output_weight, "head", axis=0, tiled=True)
     token_count, model_width = whole.shape
     normed = norm_rows(whole.astype(jnp.float32), norm_attn).astype(jnp.bfloat16)
     counts = new_counts[0]
@@ -239,20 +240,18 @@
     nkv_win = jnp.einsum("tw,tc->wc", select, newkv, preferred_element_type=jnp.float32)
     nkv_win = nkv_win.astype(jnp.bfloat16).reshape(req_n, WIN, width)
     out_win = attention(counts, q_win, kv_cache, nkv_win)
-    out_win = out_win.reshape(groups, req_n * WIN, width)
+    out_win = out_win[..., head_size:].reshape(groups, req_n * WIN, head_size)
     attn_rows = jnp.einsum("tw,gwc->gtc", select, out_win, preferred_element_type=jnp.float32)
     attn_rows = attn_rows.astype(jnp.bfloat16)
-    o_weight = output_weight.reshape(groups, head_size, model_width)
-    o_weight = jnp.concatenate([jnp.zeros_like(o_weight), o_weight], axis=1)
-
-    partial_value = jnp.einsum(
-        "gtc,gcd->td", attn_rows, o_weight, preferred_element_type=jnp.float32
-    )
+    n_head = lax.axis_size("head")
     per_block = routes.shape[0]
     row_start = lax.axis_index("head") * per_block
-    summed = lax.psum_scatter(
-        partial_value.astype(jnp.bfloat16), "head", scatter_dimension=0, tiled=True
-    ).astype(jnp.float32)
+    leaving = jnp.transpose(attn_rows.reshape(groups, n_head, per_block, head_size), (1, 0, 2, 3))
+    arriving = lax.all_to_all(leaving, "head", split_axis=0, concat_axis=0, tiled=True)
+    o_weight = o_weight_all.reshape(n_head, groups, head_size, model_width)
+    summed = jnp.einsum(
+        "hgtc,hgcd->td", arriving, o_weight, preferred_element_type=jnp.float32
+    )
     base_rows = lax.dynamic_slice_in_dim(whole, row_start, per_block, 0)
     resid = base_rows.astype(jnp.float32) + summed
     moe_in = norm_rows(resid, norm_moe).astype(jnp.bfloat16)

time: 422 us -> 388 us (0.919)
  waiting for transfers between devices: 143 us -> 96.9 us
  blocking collectives: 77.9 us -> 89.2 us
  Pallas kernels: 77 us -> 66.2 us
  starting transfers between devices: 8.33 us -> 14.4 us
  local copies, waits for them, and re-layouts: 18.9 us -> 23.3 us
    reduce_scatter x1 -> x0, waiting for transfers between devices: 24.1 us -> none  [local(): lax.psum_scatter(partial_value.astype(jnp.bfloat16), 'head', scatter_dime...]
    all_to_all x1, waiting for transfers between devices: 107 us -> 92.3 us  [local(): lax.all_to_all(produced, 'req', split_axis=0, concat_axis=0, tiled=True)]
    all_to_all x1, blocking collectives: 77.9 us -> 89.2 us  [local(): lax.all_to_all(outgoing, 'req', split_axis=0, concat_axis=0, tiled=True)]
    pallas_call x1, Pallas kernels: 77 us -> 66.2 us  [attention(): pl.pallas_call(attn_kernel, grid_spec=grid_spec, out_shape=jax.ShapeDtype...]
    all_gather x1, waiting for transfers between devices: 10.9 us -> 3.16 us  [local(): whole = lax.all_gather(tokens, 'head', axis=1, tiled=True)]
    all_to_all x0 -> x1, starting transfers between devices: none -> 5.68 us  [local(): lax.all_to_all(leaving, 'head', split_axis=0, concat_axis=0, tiled=True)]
  transfers between devices with their start and end apart: 3 -> 4, of which waited for: 3 -> 2; matrix products, arithmetic and copies ran while one was open for 8% -> 18% of each run, Pallas kernels for 0% -> 17%
where the time goes in v4:
time: 388 us; the launch traced here: 385 us
  waiting for transfers between devices  96.9 us (25%)
  blocking collectives  89.2 us (23%)
  Pallas kernels  66.2 us (17%)
  matrix products  58.3 us (15%)
  local copies, waits for them, and re-layouts  23.3 us (6%)
  other arithmetic  23.1 us (6%)
  starting transfers between devices  14.4 us (4%)
  between operations  13.6 us (4%)
    all_to_all x1, waiting for transfers between devices, local(): lax.all_to_all(produced, 'req', split_axis=0, concat_axis=0, tiled=True)  92.3 us
    all_to_all x1, blocking collectives, local(): lax.all_to_all(outgoing, 'req', split_axis=0, concat_axis=0, tiled=True)  89.2 us
    pallas_call x1, Pallas kernels, attention(): pl.pallas_call(attn_kernel, grid_spec=grid_spec, out_shape=jax.ShapeDtype...  66.2 us
    dot_general x1, matrix products, local(): jnp.einsum('sncd,ndf->sncf', lax.all_to_all(outgoing, 'req', split_axis=0...  8.82 us
    all_to_all x1, starting transfers between devices, local(): lax.all_to_all(produced, 'req', split_axis=0, concat_axis=0, tiled=True)  8.66 us
  transfers between devices with their start and end apart: 4, of which 2 were waited for; matrix products, arithmetic and copies ran while one was open for 18% of the time, Pallas kernels for 17%

profile of v4, /device:TPU:124, one launch (start us, length us, event | category | flops | bytes accessed | tf_op | source)
XLA Modules:
  0.0 385.0 jit_solution(9291416880257661254)
XLA Ops:
  6.5 0.7 all-gather.3.cloned.1.call-update
  7.3 0.7 all-gather.5.cloned.1.call-update
  8.0 0.8 reduce-window.4
  8.9 0.7 fusion.109
  9.6 0.8 select_reduce_fusion.2
  10.6 3.2 fusion.93
  13.8 1.9 copy.93
  15.7 1.9 copy.94
  17.7 1.8 concatenate.26.clone
  19.5 1.8 concatenate.28.clone
  21.4 0.6 add.121
  22.6 0.7 copy.77
  23.3 0.9 eq.73
  24.9 0.7 convert_element_type.105
  25.6 0.9 copy.78
  26.5 0.7 multiply_add_fusion
  27.2 0.7 copy.79
  28.0 0.6 pad.10.clone
  28.6 1.3 iota_compare_fusion.9
  29.9 0.7 iota_add_fusion
  30.5 1.9 slice_negate_fusion.1
  32.5 1.0 slice_negate_fusion
  33.5 3.2 all-gather.3.cloned.1.call-done
  36.7 2.6 fusion.11
  39.3 0.6 copy-done.11
  39.9 4.8 %fusion.32 = f32[3,128,1024]{2,1,0:T(8,128)} fusion(bf16[1536,3,32]{0,2,1:T(8,128)(2,1)} %get-tuple-element.8, bf16[1536,3,32]{0,2,1:T(8,128)(2,1)} %get-tuple-element.7, bf16[128]{0:T(256)(128)(2,1)} %pad.10.clone, bf16[1024,1536]{0,1:T(8,128)(2,1)} %all-gather.3.cloned.1.call-done, f32[1536]{0:T(1024)} %param.15, f32[1024]{0:T(1024)S(1)} %add_rsqrt_fusion), kind=kOutput, calls=%fused_computation.34 | convolution fusion | flops 1217789952 | bytes 5318912 | tf_op jit(solution)/shard_map/td,dgc->gtc/dot_general | solution.py:217
  44.7 7.4 %fusion.39 = bf16[3,2048,128]{1,2,0:T(8,128)(2,1)} fusion(s32[2048]{0:T(1024)S(1)} %copy-done.9, pred[2048]{0:T(1024)(128)(4,1)} %lt.29, f32[3,128,1024]{2,1,0:T(8,128)} %fusion.32, bf16[1536,3,64]{0,2,1:T(8,128)(2,1)} %bitcast.123, f32[1024,128]{0,1:T(8,128)} %concatenate.28.clone, f32[1024,128]{0,1:T(8,128)} %concatenate.26.clone, ...), kind=kOutput, calls=%fused_computation.39 | convolution fusion | flops 2831417344 | bytes 7950336 | tf_op jit(solution)/shard_map/tw,gtc->gwc/dot_general | solution.py:238
  52.1 2.6 copy.72
  54.7 4.7 %convolution_multiply_fusion = f32[1024,128]{1,0:T(8,128)} fusion(f32[1024,64]{1,0:T(8,128)} %get-tuple-element.12, bf16[1536,32]{1,0:T(8,128)(2,1)} %get-tuple-element.14, bf16[1536,32]{1,0:T(8,128)(2,1)} %get-tuple-element.13, bf16[128]{0:T(256)(128)(2,1)} %pad.10.clone, bf16[1024,1536]{0,1:T(8,128)(2,1)} %all-gather.3.cloned.1.call-done, ...), kind=kOutput, calls=%fused_computation.54 | convolution fusion | flops 410255360 | bytes 4139264 | tf_op jit(solution)/shard_map/dot_general | solution.py:229
  59.4 6.8 %fusion.50 = bf16[2048,128]{1,0:T(8,128)(2,1)} fusion(s32[2048]{0:T(1024)S(1)} %copy-done.9, pred[2048]{0:T(1024)(128)(4,1)} %lt.29, f32[1024,128]{1,0:T(8,128)} %convolution_multiply_fusion, f32[1024,64]{1,0:T(8,128)} %get-tuple-element.9, bf16[1536,1,128]{2,0,1:T(8,128)(2,1)S(1)} %copy-done.4, bf16[1024,1536]{0,1:T(8,128)(2,1)} %all-gather.3.cloned.1.call-done, ...), kind=kOutput, calls=%fused_computation.45 | convolution fusion | flops 950665216 | bytes 4870144 | tf_op jit(solution)/shard_map/tw,tc->wc/dot_general | solution.py:240
  66.2 66.2 %shard_map.118 = bf16[3,4,512,128]{3,2,1,0:T(8,128)(2,1)} custom-call(s32[4]{0:T(128)} %bitcast.132, bf16[3,4,512,128]{3,2,1,0:T(8,128)(2,1)} %bitcast.120, bf16[4,1,7680,128]{3,2,1,0:T(8,128)(2,1)} %kv_ref.1, bf16[4,512,128]{2,1,0:T(8,128)(2,1)} %bitcast.124), custom_call_target="tpu_custom_call" | custom-call | tf_op jit(solution)/shard_map/pallas_call | solution.py:167
  132.4 4.0 %fusion.73 = bf16[3,8,8,8,128]{4,3,2,1,0:T(8,128)(2,1)S(1)} fusion(s32[4,512]{1,0:T(4,128)S(1)} %iota_add_fusion, pred[4,512]{1,0:T(4,128)(4,1)S(1)} %copy-done.13, bf16[3,4,512,128]{3,2,1,0:T(8,128)(2,1)} %shard_map.118), kind=kOutput, calls=%fused_computation.60 | convolution fusion | flops 809697280 | bytes 1976320 | tf_op jit(solution)/shard_map/tw,gwc->gtc/dot_general | solution.py:244
  136.4 0.9 copy.114
  137.3 5.7 %all-to-all-start = ((bf16[8,3,128,64]{2,3,1,0:T(8,128)(2,1)}), bf16[8,3,128,64]{2,3,1,0:T(8,128)(2,1)}, u32[]{:S(2)}, u32[]{:S(2)}) async-start(bf16[8,3,128,64]{2,3,1,0:T(8,128)(2,1)} %bitcast.118), calls=%async_computation | async-start | bytes 786432 | tf_op jit(solution)/shard_map/all_to_all | solution.py:250
  143.0 4.0 %fusion = pred[128,2048]{1,0:T(8,128)(4,1)S(1)} fusion(s32[128,8]{1,0:T(8,128)S(1)} %copy-done.5), kind=kLoop, calls=%fused_computation.2 | loop fusion | flops 3932160 | bytes 266240 | tf_op jit(solution)/shard_map/reduce_or | solution.py:279
  146.9 1.8 constant_dynamic-slice_fusion
  148.7 1.9 copy.92
  150.7 3.4 multiply_reduce_fusion
  154.1 1.9 convolution_convert_fusion
  156.0 89.2 %all_to_all.15 = bf16[16,2,64,1536]{3,2,1,0:T(8,128)(2,1)S(1)} all-to-all(bf16[16,2,64,1536]{3,2,1,0:T(8,128)(2,1)S(1)} %bitcast.119), channel_id=1, replica_groups=mesh['req'=16,'head'=8] {'req'}, dimensions={0} | all-to-all | bytes 12582912 | tf_op jit(solution)/shard_map/all_to_all | solution.py:292
  245.2 8.8 %fusion.26 = f32[16,2,64,1024]{3,2,0,1:T(8,128)} fusion(bf16[2,1536,1024]{2,1,0:T(8,128)(2,1)S(1)} %bitcast.136, bf16[16,2,64,1536]{3,2,1,0:T(8,128)(2,1)S(1)} %all_to_all.15), kind=kOutput, calls=%fused_computation.32 | convolution fusion | flops 6442450944 | bytes 20971520 | tf_op jit(solution)/shard_map/sncd,ndf->sncf/dot_general | solution.py:290
  254.1 7.3 %convert_bitcast_fusion = bf16[16,2,64,1536]{3,2,0,1:T(8,128)(2,1)S(1)} fusion(bf16[2,512,1536]{2,1,0:T(8,128)(2,1)S(1)} %copy-done, f32[16,2,64,1024]{3,2,0,1:T(8,128)} %fusion.26), kind=kOutput, calls=%fused_computation.21 | convolution fusion | flops 3230662656 | bytes 17825792 | tf_op jit(solution)/shard_map/sncf,nfd->sncd/dot_general | solution.py:297
  261.3 3.1 copy.82
  264.5 8.7 %all-to-all-start.2 = ((bf16[16,2,64,1536]{3,2,1,0:T(8,128)(2,1)}), bf16[16,2,64,1536]{3,2,1,0:T(8,128)(2,1)}, u32[]{:S(2)}, u32[]{:S(2)}) async-start(bf16[16,2,64,1536]{3,2,1,0:T(8,128)(2,1)} %copy.82), calls=%async_computation.2 | async-start | bytes 12582912 | tf_op jit(solution)/shard_map/all_to_all | solution.py:300
  273.2 3.8 select_reduce_fusion
  277.0 92.3 %all-to-all-done.2 = bf16[16,2,64,1536]{3,2,1,0:T(8,128)(2,1)} async-done(((bf16[16,2,64,1536]{3,2,1,0:T(8,128)(2,1)}), bf16[16,2,64,1536]{3,2,1,0:T(8,128)(2,1)}, u32[]{:S(2)}, u32[]{:S(2)}) %all-to-all-start.2) | async-done | bytes 6291488 | tf_op jit(solution)/shard_map/all_to_all | solution.py:300
  369.3 4.2 %fusion.102 = f32[128,1536]{1,0:T(8,128)S(1)} fusion(bf16[2048,1536]{1,0:T(8,128)(2,1)} %bitcast.34, f32[128,2048]{1,0:T(8,128)} %select_reduce_fusion), kind=kOutput, calls=%fused_computation.90 | convolution fusion | flops 805568512 | bytes 8126464 | tf_op jit(solution)/shard_map/dot_general | solution.py:302
  373.5 4.6 %fusion.49 = bf16[128,1536]{1,0:T(8,128)(2,1)} fusion(f32[128,1536]{1,0:T(8,128)S(1)} %copy-done.3, f32[128,1536]{1,0:T(8,128)S(1)} %fusion.102, bf16[2048,1536]{1,0:T(8,128)(2,1)} %bitcast.34, f32[128,2048]{1,0:T(8,128)S(1)} %copy-done.1), kind=kOutput, calls=%fused_computation.44 | convolution fusion | flops 806944768 | bytes 9306112 | tf_op jit(solution)/shard_map/dot_general | solution.py:302
  (54 shorter events, 1.9 us)
Async XLA Ops:
  6.5 247.5 %copy-start = (bf16[2,512,1536]{2,1,0:T(8,128)(2,1)S(1)}, bf16[2,512,1536]{2,1,0:T(8,128)(2,1)}, u32[]{:S(2)}) copy-start(bf16[2,512,1536]{2,1,0:T(8,128)(2,1)} %param.23) | copy-start | bytes 9437188
  6.5 14.8 %copy-start.8 = (s32[1,4]{1,0:T(1,128)S(1)}, s32[1,4]{1,0:T(1,128)}, u32[]{:S(2)}) copy-start(s32[1,4]{1,0:T(1,128)} %param.13) | copy-start | bytes 52
  6.5 16.1 %copy-start.6 = (s32[128,8]{0,1:T(8,128)S(1)}, s32[128,8]{0,1:T(8,128)}, u32[]{:S(2)}) copy-start(s32[128,8]{0,1:T(8,128)} %param.20) | copy-start | bytes 12292
  6.5 30.1 %all-gather.3.cloned.1.call-start = ((), (), s32[]{:S(2)}) async-start(), calls=%async_computation.3 | async-start | bytes 3538944 | tf_op jit(solution)/shard_map/all_gather | solution.py:196
  7.3 143.4 %all-gather.5.cloned.1.call-start = ((), (), s32[]{:S(2)}) async-start(), calls=%async_computation.4 | async-start | bytes 5308416 | tf_op jit(solution)/shard_map/all_gather | solution.py:197
  10.6 21.9 %copy-start.4 = (bf16[1536,1,128]{2,0,1:T(8,128)(2,1)S(1)}, bf16[1536,1,128]{2,0,1:T(8,128)(2,1)}, u32[]{:S(2)}) copy-start(bf16[1536,1,128]{2,0,1:T(8,128)(2,1)} %param.17) | copy-start | bytes 1179652
  21.3 0.8 copy-start.12
  39.3 0.6 copy-start.11
  39.9 4.8 %copy-start.9 = (s32[2048]{0:T(1024)S(1)}, s32[2048]{0:T(1024)}, u32[]{:S(2)}) copy-start(s32[2048]{0:T(1024)} %add.121) | copy-start | bytes 24580
  66.2 66.2 %copy-start.13 = (pred[4,512]{1,0:T(4,128)(4,1)S(1)}, pred[4,512]{1,0:T(4,128)(4,1)}, u32[]{:S(2)}) copy-start(pred[4,512]{1,0:T(4,128)(4,1)} %iota_compare_fusion.9) | copy-start | bytes 6148
  132.4 10.6 %copy-start.5 = (s32[128,8]{1,0:T(8,128)S(1)}, s32[128,8]{1,0:T(8,128)}, u32[]{:S(2)}) copy-start(s32[128,8]{1,0:T(8,128)} %copy.79) | copy-start | bytes 12292
  137.3 13.4 %all-to-all-start = ((bf16[8,3,128,64]{2,3,1,0:T(8,128)(2,1)}), bf16[8,3,128,64]{2,3,1,0:T(8,128)(2,1)}, u32[]{:S(2)}, u32[]{:S(2)}) async-start(bf16[8,3,128,64]{2,3,1,0:T(8,128)(2,1)} %bitcast.118), calls=%async_computation | async-start | bytes 786432 | tf_op jit(solution)/shard_map/all_to_all | solution.py:250
  143.0 11.2 %copy-start.7 = (f32[1536]{0:T(1024)S(1)}, f32[1536]{0:T(1024)}, u32[]{:S(2)}) copy-start(f32[1536]{0:T(1024)} %param.19) | copy-start | bytes 18436
  154.1 1.9 copy-start.2
  154.1 91.1 %slice-start = ((s8[6291456]{0:T(1024)(128)(4,1)}), s8[4194304]{0:T(1024)(128)(4,1)S(1)}, s32[]{:S(2)}) async-start(s8[6291456]{0:T(1024)(128)(4,1)} %bitcast.135), calls=%async_computation.5 | async-start | bytes 8388608
  156.0 89.2 %slice-start.1 = ((s8[6291456]{0:T(1024)(128)(4,1)}), s8[2097152]{0:T(1024)(128)(4,1)S(1)}, s32[]{:S(2)}) async-start(s8[6291456]{0:T(1024)(128)(4,1)} %bitcast.135), calls=%async_computation.6 | async-start | bytes 4194304
  264.5 8.7 %copy-start.10 = (f32[128,8]{0,1:T(8,128)S(1)}, f32[128,8]{0,1:T(8,128)}, u32[]{:S(2)}) copy-start(f32[128,8]{0,1:T(8,128)} %param.21) | copy-start | bytes 12292
  264.5 104.8 %all-to-all-start.2 = ((bf16[16,2,64,1536]{3,2,1,0:T(8,128)(2,1)}), bf16[16,2,64,1536]{3,2,1,0:T(8,128)(2,1)}, u32[]{:S(2)}, u32[]{:S(2)}) async-start(bf16[16,2,64,1536]{3,2,1,0:T(8,128)(2,1)} %copy.82), calls=%async_computation.2 | async-start | bytes 12582912 | tf_op jit(solution)/shard_map/all_to_all | solution.py:300
  369.3 4.2 %copy-start.1 = (f32[128,2048]{1,0:T(8,128)S(1)}, f32[128,2048]{1,0:T(8,128)}, u32[]{:S(2)}) copy-start(f32[128,2048]{1,0:T(8,128)} %select_reduce_fusion) | copy-start | bytes 3145732
  369.3 4.2 %copy-start.3 = (f32[128,1536]{1,0:T(8,128)S(1)}, f32[128,1536]{1,0:T(8,128)}, u32[]{:S(2)}) copy-start(f32[128,1536]{1,0:T(8,128)} %copy-done.2) | copy-start | bytes 2359300
Sparse Core Ops, SparseCore 0:
  9.0 27.5 all-gather.2
  38.3 33.3 all-gather.4

commit v5 on v4

--- a/solution.py
+++ b/solution.py
@@ -94,37 +94,43 @@
         l_sc[...] = jnp.zeros(l_sc.shape, jnp.float32)
         acc_sc[...] = jnp.zeros(acc_sc.shape, jnp.float32)
 
-    def absorb(rows, mask):
-        q = q_ref[:, 0].reshape(groups * tq, width)
+    def absorb_group(g, rows, mask):
         s = lax.dot_general(
-            q, rows, (((1,), (1,)), ((), ())), preferred_element_type=jnp.float32
+            q_ref[g, 0], rows, (((1,), (1,)), ((), ())), preferred_element_type=jnp.float32
         )
-        s = s.reshape(groups, tq, rows.shape[0])
-        if mask is not None:
-            s = jnp.where(mask, s, floor_score)
-        m_old = m_sc[...]
+        s = jnp.where(mask, s, floor_score)
+        m_old = m_sc[g]
         m_new = jnp.maximum(m_old, jnp.max(s, axis=-1, keepdims=True))
         alpha = jnp.exp(m_old - m_new)
         p = jnp.exp(s - m_new)
-        l_sc[...] = l_sc[...] * alpha + jnp.sum(p, axis=-1, keepdims=True)
-        pv = jnp.dot(
-            p.astype(jnp.bfloat16).reshape(groups * tq, rows.shape[0]),
-            rows,
-            preferred_element_type=jnp.float32,
-        )
-        acc_sc[...] = acc_sc[...] * alpha + pv.reshape(groups, tq, width)
-        m_sc[...] = m_new
+        l_sc[g] = l_sc[g] * alpha + jnp.sum(p, axis=-1, keepdims=True)
+        pv = jnp.dot(p.astype(jnp.bfloat16), rows, preferred_element_type=jnp.float32)
+        acc_sc[g] = acc_sc[g] * alpha + pv
+        m_sc[g] = m_new
 
     @pl.when(tile_ok & (kb == 0))
     def _():
-        row = qi * tq + lax.broadcasted_iota(jnp.int32, (1, tq, win), 1)
-        col = lax.broadcasted_iota(jnp.int32, (1, tq, win), 2)
-        absorb(nkv_ref[0], col <= row)
+        row = qi * tq + lax.broadcasted_iota(jnp.int32, (tq, win), 0)
+        col = lax.broadcasted_iota(jnp.int32, (tq, win), 1)
+
+        def one_group(g, carry):
+            absorb_group(g, nkv_ref[0], col <= row)
+            return carry
+
+        lax.fori_loop(0, groups, one_group, 0)
 
     @pl.when(tile_ok & (kb > 0) & ((kb - 1) * tk < cached))
     def _():
-        col = (kb - 1) * tk + lax.broadcasted_iota(jnp.int32, (1, 1, tk), 2)
-        absorb(kv_ref[0, 0], col < cached)
+        pieces = tk // win
+
+        def one_piece(step, carry):
+            g = step // pieces
+            at = (step % pieces) * win
+            col = (kb - 1) * tk + at + lax.broadcasted_iota(jnp.int32, (1, win), 1)
+            absorb_group(g, kv_ref[0, 0, pl.ds(pl.multiple_of(at, win), win), :], col < cached)
+            return carry
+
+        lax.fori_loop(0, groups * pieces, one_piece, 0)
 
     @pl.when(kb == last)
     def _():

time: 388 us -> 448 us (1.15)
  Pallas kernels: 66.2 us -> 140 us
  blocking collectives: 89.2 us -> 76.4 us
    pallas_call x1, Pallas kernels: 66.2 us -> 140 us  [attention(): pl.pallas_call(attn_kernel, grid_spec=grid_spec, out_shape=jax.ShapeDtype...]
    all_to_all x1, blocking collectives: 89.2 us -> 76.4 us  [local(): lax.all_to_all(outgoing, 'req', split_axis=0, concat_axis=0, tiled=True)]
  transfers between devices with their start and end apart: 4 -> 4, of which waited for: 2 -> 2; matrix products, arithmetic and copies ran while one was open for 18% -> 16% of each run, Pallas kernels for 17% -> 32%
where the time goes in v5:
time: 448 us; the launch traced here: 445 us
  Pallas kernels  140 us (31%)
  waiting for transfers between devices  95.8 us (21%)
  blocking collectives  76.4 us (17%)
  matrix products  58.3 us (13%)
  local copies, waits for them, and re-layouts  23.3 us (5%)
  other arithmetic  23.1 us (5%)
  starting transfers between devices  14.4 us (3%)
  between operations  13.6 us (3%)
    pallas_call x1, Pallas kernels, attention(): pl.pallas_call(attn_kernel, grid_spec=grid_spec, out_shape=jax.ShapeDtype...  140 us
    all_to_all x1, waiting for transfers between devices, local(): lax.all_to_all(produced, 'req', split_axis=0, concat_axis=0, tiled=True)  91.2 us
    all_to_all x1, blocking collectives, local(): lax.all_to_all(outgoing, 'req', split_axis=0, concat_axis=0, tiled=True)  76.4 us
  transfers between devices with their start and end apart: 4, of which 2 were waited for; matrix products, arithmetic and copies ran while one was open for 16% of the time, Pallas kernels for 32%

profile of v5, /device:TPU:124, one launch (start us, length us, event | category | flops | bytes accessed | tf_op | source)
XLA Modules:
  0.0 445.2 jit_solution(6709626663037257244)
XLA Ops:
  6.5 0.7 all-gather.3.cloned.1.call-update
  7.3 0.7 all-gather.5.cloned.1.call-update
  8.0 0.8 reduce-window.4
  8.9 0.7 fusion.109
  9.6 0.8 select_reduce_fusion.2
  10.6 3.2 fusion.93
  13.8 1.9 copy.93
  15.7 1.9 copy.94
  17.7 1.8 concatenate.26.clone
  19.5 1.8 concatenate.28.clone
  21.4 0.6 add.121
  22.6 0.7 copy.77
  23.3 0.9 eq.73
  24.9 0.7 convert_element_type.105
  25.6 0.9 copy.78
  26.5 0.7 multiply_add_fusion
  27.2 0.7 copy.79
  28.0 0.6 pad.10.clone
  28.6 1.3 iota_compare_fusion.9
  29.9 0.7 iota_add_fusion
  30.5 1.9 slice_negate_fusion.1
  32.5 1.0 slice_negate_fusion
  33.5 3.2 all-gather.3.cloned.1.call-done
  36.7 2.6 fusion.11
  39.3 0.6 copy-done.11
  39.9 4.8 %fusion.32 = f32[3,128,1024]{2,1,0:T(8,128)} fusion(bf16[1536,3,32]{0,2,1:T(8,128)(2,1)} %get-tuple-element.8, bf16[1536,3,32]{0,2,1:T(8,128)(2,1)} %get-tuple-element.7, bf16[128]{0:T(256)(128)(2,1)} %pad.10.clone, bf16[1024,1536]{0,1:T(8,128)(2,1)} %all-gather.3.cloned.1.call-done, f32[1536]{0:T(1024)} %param.15, f32[1024]{0:T(1024)S(1)} %add_rsqrt_fusion), kind=kOutput, calls=%fused_computation.34 | convolution fusion | flops 1217789952 | bytes 5318912 | tf_op jit(solution)/shard_map/td,dgc->gtc/dot_general | solution.py:223
  44.7 7.4 %fusion.39 = bf16[3,2048,128]{1,2,0:T(8,128)(2,1)} fusion(s32[2048]{0:T(1024)S(1)} %copy-done.9, pred[2048]{0:T(1024)(128)(4,1)} %lt.29, f32[3,128,1024]{2,1,0:T(8,128)} %fusion.32, bf16[1536,3,64]{0,2,1:T(8,128)(2,1)} %bitcast.123, f32[1024,128]{0,1:T(8,128)} %concatenate.28.clone, f32[1024,128]{0,1:T(8,128)} %concatenate.26.clone, ...), kind=kOutput, calls=%fused_computation.39 | convolution fusion | flops 2831417344 | bytes 7950336 | tf_op jit(solution)/shard_map/tw,gtc->gwc/dot_general | solution.py:244
  52.1 2.6 copy.72
  54.7 4.7 %convolution_multiply_fusion = f32[1024,128]{1,0:T(8,128)} fusion(f32[1024,64]{1,0:T(8,128)} %get-tuple-element.12, bf16[1536,32]{1,0:T(8,128)(2,1)} %get-tuple-element.14, bf16[1536,32]{1,0:T(8,128)(2,1)} %get-tuple-element.13, bf16[128]{0:T(256)(128)(2,1)} %pad.10.clone, bf16[1024,1536]{0,1:T(8,128)(2,1)} %all-gather.3.cloned.1.call-done, ...), kind=kOutput, calls=%fused_computation.54 | convolution fusion | flops 410255360 | bytes 4139264 | tf_op jit(solution)/shard_map/dot_general | solution.py:235
  59.4 6.8 %fusion.50 = bf16[2048,128]{1,0:T(8,128)(2,1)} fusion(s32[2048]{0:T(1024)S(1)} %copy-done.9, pred[2048]{0:T(1024)(128)(4,1)} %lt.29, f32[1024,128]{1,0:T(8,128)} %convolution_multiply_fusion, f32[1024,64]{1,0:T(8,128)} %get-tuple-element.9, bf16[1536,1,128]{2,0,1:T(8,128)(2,1)S(1)} %copy-done.4, bf16[1024,1536]{0,1:T(8,128)(2,1)} %all-gather.3.cloned.1.call-done, ...), kind=kOutput, calls=%fused_computation.45 | convolution fusion | flops 950665216 | bytes 4870144 | tf_op jit(solution)/shard_map/tw,tc->wc/dot_general | solution.py:246
  66.2 140.3 %shard_map.118 = bf16[3,4,512,128]{3,2,1,0:T(8,128)(2,1)} custom-call(s32[4]{0:T(128)} %bitcast.132, bf16[3,4,512,128]{3,2,1,0:T(8,128)(2,1)} %bitcast.120, bf16[4,1,7680,128]{3,2,1,0:T(8,128)(2,1)} %kv_ref.1, bf16[4,512,128]{2,1,0:T(8,128)(2,1)} %bitcast.124), custom_call_target="tpu_custom_call" | custom-call | tf_op jit(solution)/shard_map/pallas_call | solution.py:173
  206.4 4.0 fusion.73
  210.5 0.9 copy.114
  211.3 5.7 %all-to-all-start = ((bf16[8,3,128,64]{2,3,1,0:T(8,128)(2,1)}), bf16[8,3,128,64]{2,3,1,0:T(8,128)(2,1)}, u32[]{:S(2)}, u32[]{:S(2)}) async-start(bf16[8,3,128,64]{2,3,1,0:T(8,128)(2,1)} %bitcast.118), calls=%async_computation | async-start | bytes 786432 | tf_op jit(solution)/shard_map/all_to_all | solution.py:256
  217.0 4.0 fusion
  221.0 1.8 constant_dynamic-slice_fusion
  222.8 1.9 copy.92
  224.7 3.4 multiply_reduce_fusion
  228.2 1.9 convolution_convert_fusion
  230.1 76.4 %all_to_all.15 = bf16[16,2,64,1536]{3,2,1,0:T(8,128)(2,1)S(1)} all-to-all(bf16[16,2,64,1536]{3,2,1,0:T(8,128)(2,1)S(1)} %bitcast.119), channel_id=1, replica_groups=mesh['req'=16,'head'=8] {'req'}, dimensions={0} | all-to-all | bytes 12582912 | tf_op jit(solution)/shard_map/all_to_all | solution.py:298
  306.6 8.8 %fusion.26 = f32[16,2,64,1024]{3,2,0,1:T(8,128)} fusion(bf16[2,1536,1024]{2,1,0:T(8,128)(2,1)S(1)} %bitcast.136, bf16[16,2,64,1536]{3,2,1,0:T(8,128)(2,1)S(1)} %all_to_all.15), kind=kOutput, calls=%fused_computation.32 | convolution fusion | flops 6442450944 | bytes 20971520 | tf_op jit(solution)/shard_map/sncd,ndf->sncf/dot_general | solution.py:296
  315.4 7.3 %convert_bitcast_fusion = bf16[16,2,64,1536]{3,2,0,1:T(8,128)(2,1)S(1)} fusion(bf16[2,512,1536]{2,1,0:T(8,128)(2,1)S(1)} %copy-done, f32[16,2,64,1024]{3,2,0,1:T(8,128)} %fusion.26), kind=kOutput, calls=%fused_computation.21 | convolution fusion | flops 3230662656 | bytes 17825792 | tf_op jit(solution)/shard_map/sncf,nfd->sncd/dot_general | solution.py:303
  322.6 3.1 copy.82
  325.8 8.7 %all-to-all-start.2 = ((bf16[16,2,64,1536]{3,2,1,0:T(8,128)(2,1)}), bf16[16,2,64,1536]{3,2,1,0:T(8,128)(2,1)}, u32[]{:S(2)}, u32[]{:S(2)}) async-start(bf16[16,2,64,1536]{3,2,1,0:T(8,128)(2,1)} %copy.82), calls=%async_computation.2 | async-start | bytes 12582912 | tf_op jit(solution)/shard_map/all_to_all | solution.py:306
  334.6 3.8 select_reduce_fusion
  338.3 91.2 %all-to-all-done.2 = bf16[16,2,64,1536]{3,2,1,0:T(8,128)(2,1)} async-done(((bf16[16,2,64,1536]{3,2,1,0:T(8,128)(2,1)}), bf16[16,2,64,1536]{3,2,1,0:T(8,128)(2,1)}, u32[]{:S(2)}, u32[]{:S(2)}) %all-to-all-start.2) | async-done | bytes 6291488 | tf_op jit(solution)/shard_map/all_to_all | solution.py:306
  429.6 4.2 fusion.102
  433.8 4.6 %fusion.49 = bf16[128,1536]{1,0:T(8,128)(2,1)} fusion(f32[128,1536]{1,0:T(8,128)S(1)} %copy-done.3, f32[128,1536]{1,0:T(8,128)S(1)} %fusion.102, bf16[2048,1536]{1,0:T(8,128)(2,1)} %bitcast.34, f32[128,2048]{1,0:T(8,128)S(1)} %copy-done.1), kind=kOutput, calls=%fused_computation.44 | convolution fusion | flops 806944768 | bytes 9306112 | tf_op jit(solution)/shard_map/dot_general | solution.py:308
  (54 shorter events, 1.9 us)
Async XLA Ops:
  6.5 308.8 %copy-start = (bf16[2,512,1536]{2,1,0:T(8,128)(2,1)S(1)}, bf16[2,512,1536]{2,1,0:T(8,128)(2,1)}, u32[]{:S(2)}) copy-start(bf16[2,512,1536]{2,1,0:T(8,128)(2,1)} %param.23) | copy-start | bytes 9437188
  6.5 14.8 %copy-start.8 = (s32[1,4]{1,0:T(1,128)S(1)}, s32[1,4]{1,0:T(1,128)}, u32[]{:S(2)}) copy-start(s32[1,4]{1,0:T(1,128)} %param.13) | copy-start | bytes 52
  6.5 16.1 %copy-start.6 = (s32[128,8]{0,1:T(8,128)S(1)}, s32[128,8]{0,1:T(8,128)}, u32[]{:S(2)}) copy-start(s32[128,8]{0,1:T(8,128)} %param.20) | copy-start | bytes 12292
  6.5 30.1 %all-gather.3.cloned.1.call-start = ((), (), s32[]{:S(2)}) async-start(), calls=%async_computation.3 | async-start | bytes 3538944 | tf_op jit(solution)/shard_map/all_gather | solution.py:202
  7.3 217.5 %all-gather.5.cloned.1.call-start = ((), (), s32[]{:S(2)}) async-start(), calls=%async_computation.4 | async-start | bytes 5308416 | tf_op jit(solution)/shard_map/all_gather | solution.py:203
  10.6 21.9 %copy-start.4 = (bf16[1536,1,128]{2,0,1:T(8,128)(2,1)S(1)}, bf16[1536,1,128]{2,0,1:T(8,128)(2,1)}, u32[]{:S(2)}) copy-start(bf16[1536,1,128]{2,0,1:T(8,128)(2,1)} %param.17) | copy-start | bytes 1179652
  21.3 0.8 copy-start.12
  39.3 0.6 copy-start.11
  39.9 4.8 %copy-start.9 = (s32[2048]{0:T(1024)S(1)}, s32[2048]{0:T(1024)}, u32[]{:S(2)}) copy-start(s32[2048]{0:T(1024)} %add.121) | copy-start | bytes 24580
  66.2 140.3 %copy-start.13 = (pred[4,512]{1,0:T(4,128)(4,1)S(1)}, pred[4,512]{1,0:T(4,128)(4,1)}, u32[]{:S(2)}) copy-start(pred[4,512]{1,0:T(4,128)(4,1)} %iota_compare_fusion.9) | copy-start | bytes 6148
  206.4 10.6 %copy-start.5 = (s32[128,8]{1,0:T(8,128)S(1)}, s32[128,8]{1,0:T(8,128)}, u32[]{:S(2)}) copy-start(s32[128,8]{1,0:T(8,128)} %copy.79) | copy-start | bytes 12292
  211.3 13.4 %all-to-all-start = ((bf16[8,3,128,64]{2,3,1,0:T(8,128)(2,1)}), bf16[8,3,128,64]{2,3,1,0:T(8,128)(2,1)}, u32[]{:S(2)}, u32[]{:S(2)}) async-start(bf16[8,3,128,64]{2,3,1,0:T(8,128)(2,1)} %bitcast.118), calls=%async_computation | async-start | bytes 786432 | tf_op jit(solution)/shard_map/all_to_all | solution.py:256
  217.0 11.2 %copy-start.7 = (f32[1536]{0:T(1024)S(1)}, f32[1536]{0:T(1024)}, u32[]{:S(2)}) copy-start(f32[1536]{0:T(1024)} %param.19) | copy-start | bytes 18436
  228.2 1.9 copy-start.2
  228.2 78.4 %slice-start = ((s8[6291456]{0:T(1024)(128)(4,1)}), s8[4194304]{0:T(1024)(128)(4,1)S(1)}, s32[]{:S(2)}) async-start(s8[6291456]{0:T(1024)(128)(4,1)} %bitcast.135), calls=%async_computation.5 | async-start | bytes 8388608
  230.1 76.5 %slice-start.1 = ((s8[6291456]{0:T(1024)(128)(4,1)}), s8[2097152]{0:T(1024)(128)(4,1)S(1)}, s32[]{:S(2)}) async-start(s8[6291456]{0:T(1024)(128)(4,1)} %bitcast.135), calls=%async_computation.6 | async-start | bytes 4194304
  325.8 8.7 %copy-start.10 = (f32[128,8]{0,1:T(8,128)S(1)}, f32[128,8]{0,1:T(8,128)}, u32[]{:S(2)}) copy-start(f32[128,8]{0,1:T(8,128)} %param.21) | copy-start | bytes 12292
  325.8 103.8 %all-to-all-start.2 = ((bf16[16,2,64,1536]{3,2,1,0:T(8,128)(2,1)}), bf16[16,2,64,1536]{3,2,1,0:T(8,128)(2,1)}, u32[]{:S(2)}, u32[]{:S(2)}) async-start(bf16[16,2,64,1536]{3,2,1,0:T(8,128)(2,1)} %copy.82), calls=%async_computation.2 | async-start | bytes 12582912 | tf_op jit(solution)/shard_map/all_to_all | solution.py:306
  429.6 4.2 copy-start.1
  429.6 4.2 copy-start.3
Sparse Core Ops, SparseCore 0:
  9.0 27.5 all-gather.2
  38.3 33.3 all-gather.4
